TPU v7x, 256 devices: a whole 4x4x8 slice. The times are simulated.
256 devices in a mesh: rcv: 16 (over z, core), twin: 16 (over x, y).
Axes of the slice: x: 4, y: 4, z: 8, core: 2. Of those that a mesh axis runs over, the one named last changes fastest.
Arguments:
- record: bfloat16 [4096, 8, 8192], P('rcv', None, 'twin'), may hold values from -6 to 6
- slip_block: int32 [64], P('twin'), may hold values from 16 to 127, as said below
- ghost_lag: int32 [64, 4], P('twin'), may hold values from 1 to 143, as said below
- order_ops: bfloat16 [4, 512, 512], replicated, may hold values from -0.25 to 0.25
Outputs:
- denoised: bfloat16 [4096, 8, 8192], P('rcv', None, 'twin')
Inputs may be any that keep to these rules, and one draw needn't show every extreme that they name: `slip_block`: record r begins in a block b with b mod 16 = r // 4 and b // 16 >= 1; the 4 records of one twin index begin in distinct blocks. `ghost_lag`: among the records of one twin index, at most 2 pairs (r, h) with landing >= 0 land on blocks of one twin index; some twin index receives exactly 2 such pairs from every twin index.
All inputs are finite; a program needn't handle non-finite values.
Results may differ from a plain program's by a relative error of at most 0.009.
Values may be sent and summed in bfloat16 or wider, within the bound.
No kernel may reach another device: no remote copies, remote signals or barrier semaphores. Data moves between devices by JAX's collectives and lax.ppermute only.
A program may use at most 128 MiB of HBM per device.

v0:
```python
import jax
import jax.numpy as jnp
from jax import lax
from jax.sharding import PartitionSpec as P


def with_halo(block, sides, width):
    for axis, dim in sides:
        count = lax.axis_size(axis)
        forward = [(i, i + 1) for i in range(count - 1)]
        backward = [(target, source) for source, target in forward]
        low = lax.ppermute(
            lax.slice_in_dim(block, block.shape[dim] - width, None, axis=dim), axis, forward
        )
        high = lax.ppermute(lax.slice_in_dim(block, 0, width, axis=dim), axis, backward)
        block = jnp.concatenate([low, block, high], axis=dim)
    return block


def landing_slots(slip_block, ghost_lag, twin_count):
    rec_count, order_count = ghost_lag.shape
    pair_total = rec_count * order_count
    slot_count = pair_total // twin_count + 1
    target = slip_block[:, None] - ghost_lag
    valid = target >= 0
    safe = jnp.maximum(target, 0)
    owner = jnp.where(valid, safe % twin_count, -1).reshape(pair_total)
    land_round = (safe // twin_count).reshape(pair_total)
    order_id = jnp.broadcast_to(
        jnp.arange(order_count, dtype=jnp.int32)[None, :], (rec_count, order_count)
    ).reshape(pair_total)
    position = jnp.arange(pair_total, dtype=jnp.int32)
    earlier = (owner[None, :] == owner[:, None]) & (position[None, :] < position[:, None])
    slot = jnp.sum(earlier.astype(jnp.int32), axis=1)
    chosen = (owner[:, None, None] == jnp.arange(twin_count, dtype=jnp.int32)[None, :, None]) & (
        slot[:, None, None] == jnp.arange(slot_count, dtype=jnp.int32)[None, None, :]
    )
    chosen_int = chosen.astype(jnp.int32)
    landed = jnp.sum(chosen_int * (land_round + 1)[:, None, None], axis=0) - 1
    orders = jnp.sum(chosen_int * (order_id + 1)[:, None, None], axis=0) - 1
    selector = chosen.astype(jnp.bfloat16).reshape(rec_count, order_count, twin_count, slot_count)
    return (selector, landed, orders)


def place_slots(arrived, arrived_rounds, rounds):
    hit = (arrived_rounds[:, :, None] == jnp.arange(rounds, dtype=jnp.int32)[None, None, :]).astype(
        jnp.bfloat16
    )
    return jnp.einsum("nsr,nscp->crp", hit, arrived, preferred_element_type=jnp.float32)


def local(record, slip_block, ghost_lag, order_ops):
    twin_count = lax.axis_size("twin")
    channels, rounds, samples = record.shape
    guides = jnp.moveaxis(jnp.take(record, slip_block // twin_count, axis=1), 1, 0)
    selector, landed, orders = landing_slots(slip_block, ghost_lag, twin_count)
    outgoing = jnp.einsum(
        "jhns,jcp->nscp", selector, guides, preferred_element_type=jnp.float32
    ).astype(jnp.bfloat16)
    panels = lax.all_to_all(outgoing, "twin", split_axis=0, concat_axis=0, tiled=True)
    panel_rounds = lax.all_to_all(landed, "twin", split_axis=0, concat_axis=0, tiled=True)
    panel_orders = lax.all_to_all(orders, "twin", split_axis=0, concat_axis=0, tiled=True)

    def one_source(items):
        source_panels, source_orders = items
        operators = jnp.take(order_ops, jnp.maximum(source_orders, 0), axis=0)
        return jnp.einsum(
            "scp,spq->scq", source_panels, operators, preferred_element_type=jnp.float32
        ).astype(jnp.bfloat16)

    arrived = lax.map(one_source, (panels, panel_orders))
    noise = place_slots(arrived, panel_rounds, rounds)
    cleaned = (record.astype(jnp.float32) - noise).astype(jnp.bfloat16)
    padded = with_halo(cleaned, (("rcv", 0),), 1)
    widened = padded.astype(jnp.float32)
    smooth = 0.5 * widened[1:-1] + 0.25 * (widened[:-2] + widened[2:])
    return smooth.astype(jnp.bfloat16)


def solution(mesh):
    placed = (P("rcv", None, "twin"), P("twin"), P("twin", None), P())
    return jax.shard_map(
        local, mesh=mesh, in_specs=placed, out_specs=P("rcv", None, "twin"), check_vma=False
    )
```

profile of v0, /device:TPU:97, one launch (start us, length us, event | category | flops | bytes accessed | tf_op | source)
XLA Modules:
  0.0 276.4 jit_solution(15389540414267376286)
XLA Ops:
  2.1 6.8 %all-to-all-start.1 = ((s32[16,1,2]{2,1,0:T(1,128)}), s32[16,1,2]{2,1,0:T(1,128)S(1)}, u32[]{:S(2)}, u32[]{:S(2)}) async-start(s32[16,1,2]{2,1,0:T(1,128)} %copy.25), calls=%async_computation.1 | async-start | bytes 16384 | tf_op jit(solution)/shard_map/all_to_all | solution.py:62
  10.5 5.0 %gather_fusion.1 = bf16[4,256,512]{2,0,1:T(4,128)(2,1)S(1)} fusion(bf16[256,8,512]{2,1,0:T(8,128)(2,1)} %param.6, s32[1024]{0:T(1024)S(1)} %pad_clamp_fusion.1), kind=kCustom, calls=%fused_computation.1 | custom fusion | bytes 2097168 | tf_op jit(solution)/shard_map/jit(_take)/gather | solution.py:55
  15.5 6.7 %all-to-all-start.2 = ((s32[16,1,2]{2,1,0:T(1,128)}), s32[16,1,2]{2,1,0:T(1,128)S(1)}, u32[]{:S(2)}, u32[]{:S(2)}) async-start(s32[16,1,2]{2,1,0:T(1,128)} %copy.28), calls=%async_computation.2 | async-start | bytes 16384 | tf_op jit(solution)/shard_map/all_to_all | solution.py:61
  22.2 5.0 %convolution_convert_fusion.1 = bf16[16,2,256,512]{3,0,2,1:T(8,128)(2,1)} fusion(bf16[4,256,512]{2,0,1:T(4,128)(2,1)S(1)} %gather_fusion.1, pred[4]{0:T(512)(128)(4,1)S(1)} %get-tuple-element.70, bf16[4,16,2,1]{1,2,0,3:T(2,128)(2,1)S(1)} %bitcast.40), kind=kOutput, calls=%fused_computation.19 | convolution fusion | flops 34078720 | bytes 9437444 | tf_op jit(solution)/shard_map/jhns,jcp->nscp/dot_general | solution.py:57
  27.2 11.3 %copy.24 = bf16[16,2,256,512]{3,2,1,0:T(8,128)(2,1)} copy(bf16[16,2,256,512]{3,0,2,1:T(8,128)(2,1)} %convolution_convert_fusion.1) | data formatting | bytes 16777216 | tf_op jit(solution)/shard_map/convert_element_type | solution.py:59
  38.5 6.7 %all-to-all-start = ((bf16[16,2,256,512]{3,2,1,0:T(8,128)(2,1)}), bf16[16,2,256,512]{3,2,1,0:T(8,128)(2,1)}, u32[]{:S(2)}, u32[]{:S(2)}) async-start(bf16[16,2,256,512]{3,2,1,0:T(8,128)(2,1)} %copy.24), calls=%async_computation | async-start | bytes 16777216 | tf_op jit(solution)/shard_map/all_to_all | solution.py:60
  45.4 130.9 %all-to-all-done = bf16[16,2,256,512]{3,2,1,0:T(8,128)(2,1)} async-done(((bf16[16,2,256,512]{3,2,1,0:T(8,128)(2,1)}), bf16[16,2,256,512]{3,2,1,0:T(8,128)(2,1)}, u32[]{:S(2)}, u32[]{:S(2)}) %all-to-all-start) | async-done | bytes 8388640 | tf_op jit(solution)/shard_map/all_to_all | solution.py:60
  176.2 74.2 %while.10 = (s32[]{:T(128)}, bf16[16,2,256,512]{3,2,1,0:T(8,128)(2,1)}, bf16[16,2,256,512]{3,2,1,0:T(8,128)(2,1)}, s32[16,2]{1,0:T(8,128)S(1)}, bf16[4,512,512]{2,1,0:T(8,128)(2,1)}, /*index=5*/s32[]{:T(128)}) while((s32[]{:T(128)}, bf16[16,2,256,512]{3,2,1,0:T(8,128)(2,1)}, bf16[16,2,256,512]{3,2,1,0:T(8,128)(2,1)}, s32[16,2]{1,0:T(8,128)S(1)}, ...), condition=%wide.region_4.5_spmd, body=%wide.region_3.4_spmd.sunk | while | flops 269222912 | bytes 4199545 | solution.py:71
  176.3 2.4 gather_fusion
  178.6 2.4 fusion.42
  181.0 2.2 gather_fusion
  183.3 2.4 fusion.42
  185.7 2.2 gather_fusion
  187.9 2.4 fusion.42
  190.3 2.2 gather_fusion
  192.5 2.4 fusion.42
  197.1 2.4 fusion.42
  201.8 2.4 fusion.42
  206.4 2.4 fusion.42
  211.0 2.4 fusion.42
  213.4 2.2 gather_fusion
  215.6 2.4 fusion.42
  220.2 2.4 fusion.42
  224.9 2.4 fusion.42
  229.5 2.4 fusion.42
  234.2 2.4 fusion.42
  238.8 2.4 fusion.42
  243.4 2.4 fusion.42
  248.0 2.4 fusion.42
  250.5 8.3 %fusion.16 = bf16[256,8,512]{2,1,0:T(8,128)(2,1)S(1)} fusion(bf16[256,8,512]{2,1,0:T(8,128)(2,1)S(1)} %copy-done, bf16[16,2,256,512]{3,2,1,0:T(8,128)(2,1)} %get-tuple-element.32, s32[16,2]{0,1:T(2,128)S(1)} %bitcast.41), kind=kOutput, calls=%fused_computation.26 | convolution fusion | flops 70254848 | bytes 12583040 | tf_op jit(solution)/shard_map/nsr,nscp->crp/dot_general | solution.py:49
  258.8 9.1 %collective-permute-start = (bf16[1,8,512]{2,1,0:T(8,128)(2,1)S(1)}, bf16[1,8,512]{2,1,0:T(8,128)(2,1)S(1)}, u32[]{:S(2)}, u32[]{:S(2)}) collective-permute-start(bf16[1,8,512]{2,1,0:T(8,128)(2,1)S(1)} %get-tuple-element.72), channel_id=1, source_target_pairs={{0,16},{16,32},{32,48},{48,64},{64,80},{80,96},{96,112},{112,128},... | collective-permute-start | bytes 24584 | tf_op jit(solution)/shard_map/ppermute | solution.py:12
  269.8 4.2 %collective-permute-done.1 = bf16[1,8,512]{2,1,0:T(8,128)(2,1)S(1)} collective-permute-done((bf16[1,8,512]{2,1,0:T(8,128)(2,1)S(1)}, bf16[1,8,512]{2,1,0:T(8,128)(2,1)S(1)}, u32[]{:S(2)}, u32[]{:S(2)}) %collective-permute-start.1) | collective-permute-done | bytes 8224 | tf_op jit(solution)/shard_map/ppermute | solution.py:15
  (89 shorter events, 32.8 us)
Async XLA Ops:
  2.1 13.4 %all-to-all-start.1 = ((s32[16,1,2]{2,1,0:T(1,128)}), s32[16,1,2]{2,1,0:T(1,128)S(1)}, u32[]{:S(2)}, u32[]{:S(2)}) async-start(s32[16,1,2]{2,1,0:T(1,128)} %copy.25), calls=%async_computation.1 | async-start | bytes 16384 | tf_op jit(solution)/shard_map/all_to_all | solution.py:62
  15.5 23.1 %all-to-all-start.2 = ((s32[16,1,2]{2,1,0:T(1,128)}), s32[16,1,2]{2,1,0:T(1,128)S(1)}, u32[]{:S(2)}, u32[]{:S(2)}) async-start(s32[16,1,2]{2,1,0:T(1,128)} %copy.28), calls=%async_computation.2 | async-start | bytes 16384 | tf_op jit(solution)/shard_map/all_to_all | solution.py:61
  38.5 137.7 %all-to-all-start = ((bf16[16,2,256,512]{3,2,1,0:T(8,128)(2,1)}), bf16[16,2,256,512]{3,2,1,0:T(8,128)(2,1)}, u32[]{:S(2)}, u32[]{:S(2)}) async-start(bf16[16,2,256,512]{3,2,1,0:T(8,128)(2,1)} %copy.24), calls=%async_computation | async-start | bytes 16777216 | tf_op jit(solution)/shard_map/all_to_all | solution.py:60
  176.2 74.2 %copy-start = (bf16[256,8,512]{2,1,0:T(8,128)(2,1)S(1)}, bf16[256,8,512]{2,1,0:T(8,128)(2,1)}, u32[]{:S(2)}) copy-start(bf16[256,8,512]{2,1,0:T(8,128)(2,1)} %param.6) | copy-start | bytes 6291460
  258.8 11.1 %collective-permute-start = (bf16[1,8,512]{2,1,0:T(8,128)(2,1)S(1)}, bf16[1,8,512]{2,1,0:T(8,128)(2,1)S(1)}, u32[]{:S(2)}, u32[]{:S(2)}) collective-permute-start(bf16[1,8,512]{2,1,0:T(8,128)(2,1)S(1)} %get-tuple-element.72), channel_id=1, source_target_pairs={{0,16},{16,32},{32,48},{48,64},{64,80},{80,96},{96,112},{112,128},... | collective-permute-start | bytes 24584 | tf_op jit(solution)/shard_map/ppermute | solution.py:12
  267.9 6.2 %collective-permute-start.1 = (bf16[1,8,512]{2,1,0:T(8,128)(2,1)S(1)}, bf16[1,8,512]{2,1,0:T(8,128)(2,1)S(1)}, u32[]{:S(2)}, u32[]{:S(2)}) collective-permute-start(bf16[1,8,512]{2,1,0:T(8,128)(2,1)S(1)} %get-tuple-element.73), channel_id=1, source_target_pairs={{16,0},{32,16},{48,32},{64,48},{80,64},{96,80},{112,96},{128,112},... | collective-permute-start | bytes 24584 | tf_op jit(solution)/shard_map/ppermute | solution.py:15
where the time goes:
time: 281 us; the launch traced here: 276 us
  waiting for transfers between devices  135 us (48%)
  local copies, waits for them, and re-layouts  53.5 us (19%)
  matrix products  51.4 us (18%)
  starting transfers between devices  31.2 us (11%)
  other arithmetic  4.79 us (2%)
    all_to_all x1, waiting for transfers between devices, local(): lax.all_to_all(outgoing, 'twin', split_axis=0, concat_axis=0, tiled=True)  131 us
    dot_general x16, matrix products, one_source(): jnp.einsum('scp,spq->scq', source_panels, operators, preferred_element_ty...  38 us
    gather x16, local copies, waits for them, and re-layouts, one_source(): operators = jnp.take(order_ops, jnp.maximum(source_orders, 0), axis=0)  35.4 us
    convert_element_type x1, local copies, waits for them, and re-layouts, local(): outgoing = jnp.einsum('jhns,jcp->nscp', selector, guides, preferred_eleme...  11.3 us
    ppermute x1, starting transfers between devices, with_halo(): lax.ppermute(lax.slice_in_dim(block, block.shape[dim] - width, None, axis...  9.11 us
    dot_general x1, matrix products, place_slots(): jnp.einsum('nsr,nscp->crp', hit, arrived, preferred_element_type=jnp.floa...  8.31 us
    all_to_all x1, starting transfers between devices, local(): lax.all_to_all(orders, 'twin', split_axis=0, concat_axis=0, tiled=True)  6.75 us
    all_to_all x1, starting transfers between devices, local(): lax.all_to_all(outgoing, 'twin', split_axis=0, concat_axis=0, tiled=True)  6.72 us
  transfers between devices with their start and end apart: 5, of which 2 were waited for; matrix products, arithmetic and copies ran while one was open for 8% of the time, Pallas kernels for 0%

commit v1 on v0

v1 whole, which is shorter than its diff:
```python
import jax
import jax.numpy as jnp
from jax import lax
from jax.sharding import PartitionSpec as P


def with_halo(block, sides, width):
    for axis, dim in sides:
        count = lax.axis_size(axis)
        forward = [(i, i + 1) for i in range(count - 1)]
        backward = [(target, source) for source, target in forward]
        low = lax.ppermute(
            lax.slice_in_dim(block, block.shape[dim] - width, None, axis=dim), axis, forward
        )
        high = lax.ppermute(lax.slice_in_dim(block, 0, width, axis=dim), axis, backward)
        block = jnp.concatenate([low, block, high], axis=dim)
    return block


def pair_routes(slip_block, ghost_lag, twin_count):
    rec_count, order_count = ghost_lag.shape
    pair_total = rec_count * order_count
    target = (slip_block[:, None] - ghost_lag).reshape(pair_total)
    valid = target >= 0
    safe = jnp.maximum(target, 0)
    owner = jnp.where(valid, safe % twin_count, -1)
    land_round = safe // twin_count
    position = jnp.arange(pair_total, dtype=jnp.int32)
    earlier = (owner[None, :] == owner[:, None]) & (position[None, :] < position[:, None])
    slot = jnp.sum(earlier.astype(jnp.int32), axis=1)
    return owner, slot, land_round


def local(record, slip_block, ghost_lag, order_ops):
    twin_count = lax.axis_size("twin")
    me = lax.axis_index("twin")
    channels, rounds, samples = record.shape
    rec_count, order_count = ghost_lag.shape
    pair_total = rec_count * order_count
    slot_count = pair_total // twin_count + 1

    table = jnp.concatenate([slip_block, ghost_lag.reshape(pair_total)])
    tables = lax.all_gather(table, "twin")

    guides = jnp.take(record, slip_block // twin_count, axis=1)
    estimates = jnp.einsum(
        "crp,hpq->rhcq", guides, order_ops, preferred_element_type=jnp.float32
    ).astype(jnp.bfloat16)
    estimates = estimates.reshape(pair_total, channels, samples)

    owner, slot, _ = pair_routes(slip_block, ghost_lag, twin_count)
    chosen = (owner[:, None, None] == jnp.arange(twin_count, dtype=jnp.int32)[None, :, None]) & (
        slot[:, None, None] == jnp.arange(slot_count, dtype=jnp.int32)[None, None, :]
    )
    outgoing = jnp.einsum(
        "kns,kcq->nscq", chosen.astype(jnp.bfloat16), estimates, preferred_element_type=jnp.float32
    ).astype(jnp.bfloat16)
    arrived = lax.all_to_all(outgoing, "twin", split_axis=0, concat_axis=0, tiled=True)

    src_slip = tables[:, :rec_count]
    src_lag = tables[:, rec_count:].reshape(twin_count, rec_count, order_count)
    src_owner, src_slot, src_round = jax.vmap(pair_routes, in_axes=(0, 0, None))(
        src_slip, src_lag, twin_count
    )
    mine = src_owner == me
    hit = (
        mine[:, :, None, None]
        & (src_slot[:, :, None, None] == jnp.arange(slot_count, dtype=jnp.int32)[None, None, :, None])
        & (src_round[:, :, None, None] == jnp.arange(rounds, dtype=jnp.int32)[None, None, None, :])
    )
    hit = jnp.sum(hit.astype(jnp.int32), axis=1).astype(jnp.bfloat16)
    noise = jnp.einsum("nsr,nscq->crq", hit, arrived, preferred_element_type=jnp.float32)

    cleaned = (record.astype(jnp.float32) - noise).astype(jnp.bfloat16)
    padded = with_halo(cleaned, (("rcv", 0),), 1)
    widened = padded.astype(jnp.float32)
    smooth = 0.5 * widened[1:-1] + 0.25 * (widened[:-2] + widened[2:])
    return smooth.astype(jnp.bfloat16)


def solution(mesh):
    placed = (P("rcv", None, "twin"), P("twin"), P("twin", None), P())
    return jax.shard_map(
        local, mesh=mesh, in_specs=placed, out_specs=P("rcv", None, "twin"), check_vma=False
    )
```

time: 281 us -> 214 us (0.76); the launches traced: 276 us -> 214 us
  blocking collectives: 0 us -> 149 us
  waiting for transfers between devices: 135 us -> 0.77 us
  matrix products: 51.4 us -> 14 us
  local copies, waits for them, and re-layouts: 53.5 us -> 24.7 us
  starting transfers between devices: 31.2 us -> 18.1 us
    unnamed x0 -> x1, blocking collectives: none -> 149 us
    all_to_all x1, waiting for transfers between devices: 131 us -> 0.01 us  [local(): lax.all_to_all(outgoing, 'twin', split_axis=0, concat_axis=0, tiled=True)]
    dot_general x18 -> x3, matrix products: 51.4 us -> 14 us  [the longest x1 8.74 us: local(): jnp.einsum('nsr,nscq->crq', hit, arrived, preferred_element_type=jnp.floa...]
    gather x17 -> x1, local copies, waits for them, and re-layouts: 40.4 us -> 4.97 us  [local(): guides = jnp.take(record, slip_block // twin_count, axis=1)]
    all_to_all x2 -> x0, starting transfers between devices: 13.5 us -> none  [the longest x1 6.75 us: local(): lax.all_to_all(orders, 'twin', split_axis=0, concat_axis=0, tiled=True)]
    convert_element_type x1, local copies, waits for them, and re-layouts: 11.3 us -> 18.5 us  [local(): outgoing = jnp.einsum('kns,kcq->nscq', chosen.astype(jnp.bfloat16), estim...]
    ppermute x1, starting transfers between devices: 9.11 us -> 4.53 us  [with_halo(): lax.ppermute(lax.slice_in_dim(block, block.shape[dim] - width, None, axis...]
    ppermute x1, starting transfers between devices: 1.92 us -> 6.49 us  [with_halo(): lax.ppermute(lax.slice_in_dim(block, 0, width, axis=dim), axis, backward)]
  transfers between devices with their start and end apart: 5 -> 3, of which waited for: 2 -> 1; matrix products, arithmetic and copies ran while one was open for 8% -> 1% of each run, Pallas kernels for 0% -> 0%
where the time goes in v1:
time: 214 us
  blocking collectives  149 us (70%)
  local copies, waits for them, and re-layouts  24.7 us (12%)
  starting transfers between devices  18.1 us (8%)
  matrix products  14 us (7%)
  other arithmetic  6.89 us (3%)
    unnamed x1, blocking collectives  149 us
    convert_element_type x1, local copies, waits for them, and re-layouts, local(): outgoing = jnp.einsum('kns,kcq->nscq', chosen.astype(jnp.bfloat16), estim...  18.5 us
    dot_general x1, matrix products, local(): jnp.einsum('nsr,nscq->crq', hit, arrived, preferred_element_type=jnp.floa...  8.74 us
    all_to_all x1, starting transfers between devices, local(): lax.all_to_all(outgoing, 'twin', split_axis=0, concat_axis=0, tiled=True)  7.03 us
    ppermute x1, starting transfers between devices, with_halo(): lax.ppermute(lax.slice_in_dim(block, 0, width, axis=dim), axis, backward)  6.49 us
    gather x1, local copies, waits for them, and re-layouts, local(): guides = jnp.take(record, slip_block // twin_count, axis=1)  4.97 us
    ppermute x1, starting transfers between devices, with_halo(): lax.ppermute(lax.slice_in_dim(block, block.shape[dim] - width, None, axis...  4.53 us
  transfers between devices with their start and end apart: 3, of which 1 were waited for; matrix products, arithmetic and copies ran while one was open for 1% of the time, Pallas kernels for 0%

profile of v1, /device:TPU:97, one launch (start us, length us, event | category | flops | bytes accessed | tf_op | source)
XLA Modules:
  0.0 214.0 jit_solution(9040973383280945764)
XLA Ops:
  0.0 0.8 compare_and_fusion.1
  0.8 0.8 subtract_compare_fusion
  1.6 0.8 maximum_and_fusion
  2.3 0.1 ge.27
  2.4 0.1 rem.49
  2.5 0.2 convert_reduce_fusion.2
  2.7 0.1 iota_compare_fusion.2
  2.8 0.1 copy.31
  2.9 5.0 %gather_fusion = bf16[4,256,512]{2,0,1:T(4,128)(2,1)S(1)} fusion(bf16[256,8,512]{2,1,0:T(8,128)(2,1)} %param.4, s32[1024]{0:T(1024)S(1)} %pad_clamp_fusion), kind=kCustom, calls=%fused_computation | custom fusion | bytes 2097168 | tf_op jit(solution)/shard_map/jit(_take)/gather | solution.py:45
  7.9 0.5 select_bitcast_fusion
  8.4 2.3 %convolution_convert_fusion.1 = bf16[256,4,4,512]{3,0,2,1:T(8,128)(2,1)S(1)} fusion(bf16[4,512,512]{2,1,0:T(8,128)(2,1)S(1)} %copy-done, bf16[256,4,512,1]{2,1,0,3:T(4,128)(2,1)S(1)} %select_bitcast_fusion), kind=kOutput, calls=%fused_computation.12 | convolution fusion | flops 2149580800 | bytes 7340032 | tf_op jit(solution)/shard_map/crp,hpq->rhcq/dot_general | solution.py:46
  10.7 2.9 %convolution_convert_fusion = bf16[16,2,256,512]{3,0,1,2:T(8,128)(2,1)S(1)} fusion(bf16[16,256,512,1]{2,1,0,3:T(8,128)(2,1)S(1)} %bitcast.28, pred[16,2]{0,1:T(4,128)(4,1)S(1)} %iota_compare_fusion.3, pred[16,16]{0,1:T(8,128)(4,1)S(1)} %copy.31), kind=kOutput, calls=%fused_computation.3 | convolution fusion | flops 138412544 | bytes 12583200 | tf_op jit(solution)/shard_map/kns,kcq->nscq/dot_general | solution.py:55
  13.6 18.5 %copy.34 = bf16[16,2,256,512]{3,1,2,0:T(2,128)(2,1)} copy(bf16[16,2,256,512]{3,0,1,2:T(8,128)(2,1)S(1)} %convolution_convert_fusion) | data formatting | bytes 16777216 | tf_op jit(solution)/shard_map/convert_element_type | solution.py:57
  32.1 7.0 %all-to-all-start = ((bf16[16,2,256,512]{3,1,2,0:T(2,128)(2,1)}), bf16[16,2,256,512]{3,1,2,0:T(2,128)(2,1)}, u32[]{:S(2)}, u32[]{:S(2)}) async-start(bf16[16,2,256,512]{3,1,2,0:T(2,128)(2,1)} %copy.34), calls=%async_computation | async-start | bytes 16777216 | tf_op jit(solution)/shard_map/all_to_all | solution.py:58
  39.2 0.1 reshape.152
  39.2 0.6 dynamic-slice
  40.5 0.2 add_dynamic-update-slice_fusion
  40.7 148.8 %all-reduce = s32[320]{0:T(512)S(1)} all-reduce(s32[320]{0:T(512)S(1)} %add_dynamic-update-slice_fusion), channel_id=2, replica_groups=mesh['rcv'=16,'twin'=16] {'twin'}, use_global_device_ids=true, to_apply=%add | all-reduce | flops 320 | bytes 2560
  189.4 0.1 reshape.161
  189.5 0.1 copy.35
  189.6 0.1 copy.36
  189.7 0.1 broadcast_compare_fusion
  189.8 0.4 convert_reduce_fusion.1
  190.3 0.1 add_select_fusion
  190.4 0.6 convert_reduce_fusion
  191.0 0.1 copy.37
  191.1 8.7 %fusion.5 = bf16[256,8,512]{2,1,0:T(8,128)(2,1)S(1)} fusion(bf16[256,8,512]{2,1,0:T(8,128)(2,1)} %param.4, bf16[16,2,256,512]{3,1,2,0:T(2,128)(2,1)} %all-to-all-done, s32[16,2,8]{0,2,1:T(8,128)S(1)} %copy.37), kind=kOutput, calls=%fused_computation.10 | convolution fusion | flops 70254848 | bytes 12583936 | tf_op jit(solution)/shard_map/nsr,nscq->crq/dot_general | solution.py:72
  199.8 6.5 %collective-permute-start.1 = (bf16[1,8,512]{2,1,0:T(8,128)(2,1)S(1)}, bf16[1,8,512]{2,1,0:T(8,128)(2,1)S(1)}, u32[]{:S(2)}, u32[]{:S(2)}) collective-permute-start(bf16[1,8,512]{2,1,0:T(8,128)(2,1)S(1)} %get-tuple-element.10), channel_id=1, source_target_pairs={{16,0},{32,16},{48,32},{64,48},{80,64},{96,80},{112,96},{128,112},... | collective-permute-start | bytes 24584 | tf_op jit(solution)/shard_map/ppermute | solution.py:15
  206.3 4.5 %collective-permute-start = (bf16[1,8,512]{2,1,0:T(8,128)(2,1)S(1)}, bf16[1,8,512]{2,1,0:T(8,128)(2,1)S(1)}, u32[]{:S(2)}, u32[]{:S(2)}) collective-permute-start(bf16[1,8,512]{2,1,0:T(8,128)(2,1)S(1)} %get-tuple-element.9), channel_id=1, source_target_pairs={{0,16},{16,32},{32,48},{48,64},{64,80},{80,96},{96,112},{112,128},... | collective-permute-start | bytes 24584 | tf_op jit(solution)/shard_map/ppermute | solution.py:12
  210.9 0.8 collective-permute-done
  211.6 0.3 maximum_convert_fusion
  212.0 2.0 fusion.4
  (19 shorter events, 0.1 us)
Async XLA Ops:
  0.0 8.4 %copy-start = (bf16[4,512,512]{2,1,0:T(8,128)(2,1)S(1)}, bf16[4,512,512]{2,1,0:T(8,128)(2,1)}, u32[]{:S(2)}) copy-start(bf16[4,512,512]{2,1,0:T(8,128)(2,1)} %param.7) | copy-start | bytes 6291460
  32.1 7.1 %copy-start.1 = (s32[4,4]{1,0:T(4,128)S(1)}, s32[4,4]{1,0:T(4,128)}, u32[]{:S(2)}) copy-start(s32[4,4]{1,0:T(4,128)} %param.6) | copy-start | bytes 196
  32.1 7.2 %copy-start.3 = (u32[256]{0:T(256)S(1)}, u32[256]{0:T(256)}, u32[]{:S(2)}) copy-start(u32[256]{0:T(256)} %constant.86) | copy-start | bytes 3076
  32.1 8.4 %copy-start.2 = (s32[4]{0:T(128)S(1)}, s32[4]{0:T(128)}, u32[]{:S(2)}) copy-start(s32[4]{0:T(128)} %param.5) | copy-start | bytes 52
  32.1 159.0 %all-to-all-start = ((bf16[16,2,256,512]{3,1,2,0:T(2,128)(2,1)}), bf16[16,2,256,512]{3,1,2,0:T(2,128)(2,1)}, u32[]{:S(2)}, u32[]{:S(2)}) async-start(bf16[16,2,256,512]{3,1,2,0:T(2,128)(2,1)} %copy.34), calls=%async_computation | async-start | bytes 16777216 | tf_op jit(solution)/shard_map/all_to_all | solution.py:58
  199.8 11.0 %collective-permute-start.1 = (bf16[1,8,512]{2,1,0:T(8,128)(2,1)S(1)}, bf16[1,8,512]{2,1,0:T(8,128)(2,1)S(1)}, u32[]{:S(2)}, u32[]{:S(2)}) collective-permute-start(bf16[1,8,512]{2,1,0:T(8,128)(2,1)S(1)} %get-tuple-element.10), channel_id=1, source_target_pairs={{16,0},{32,16},{48,32},{64,48},{80,64},{96,80},{112,96},{128,112},... | collective-permute-start | bytes 24584 | tf_op jit(solution)/shard_map/ppermute | solution.py:15
  206.3 5.3 %collective-permute-start = (bf16[1,8,512]{2,1,0:T(8,128)(2,1)S(1)}, bf16[1,8,512]{2,1,0:T(8,128)(2,1)S(1)}, u32[]{:S(2)}, u32[]{:S(2)}) collective-permute-start(bf16[1,8,512]{2,1,0:T(8,128)(2,1)S(1)} %get-tuple-element.9), channel_id=1, source_target_pairs={{0,16},{16,32},{32,48},{48,64},{64,80},{80,96},{96,112},{112,128},... | collective-permute-start | bytes 24584 | tf_op jit(solution)/shard_map/ppermute | solution.py:12

commit v2 on v1

v2 whole, which is shorter than its diff:
```python
import jax
import jax.numpy as jnp
from jax import lax
from jax.sharding import PartitionSpec as P


def pair_routes(slip_block, ghost_lag, twin_count):
    rec_count, order_count = ghost_lag.shape
    pair_total = rec_count * order_count
    target = (slip_block[:, None] - ghost_lag).reshape(pair_total)
    valid = target >= 0
    safe = jnp.maximum(target, 0)
    owner = jnp.where(valid, safe % twin_count, -1)
    land_round = safe // twin_count
    position = jnp.arange(pair_total, dtype=jnp.int32)
    earlier = (owner[None, :] == owner[:, None]) & (position[None, :] < position[:, None])
    slot = jnp.sum(earlier.astype(jnp.int32), axis=1)
    return owner, slot, land_round


def local(record, slip_block, ghost_lag, order_ops):
    twin_count = lax.axis_size("twin")
    channels, rounds, samples = record.shape
    rec_count, order_count = ghost_lag.shape
    pair_total = rec_count * order_count
    slot_count = pair_total // twin_count + 1

    guides = jnp.take(record, slip_block // twin_count, axis=1, mode="clip")
    estimates = jnp.einsum(
        "crp,hpq->rhcq", guides, order_ops, preferred_element_type=jnp.float32
    ).astype(jnp.bfloat16)
    estimates = estimates.reshape(pair_total, channels, samples)

    owner, slot, land_round = pair_routes(slip_block, ghost_lag, twin_count)
    meta_rows = 8
    meta = jnp.broadcast_to(land_round.astype(jnp.bfloat16)[:, None, None], (pair_total, meta_rows, samples))
    blank = jnp.zeros((1, channels + meta_rows, samples), jnp.bfloat16)
    tagged = jnp.concatenate([jnp.concatenate([estimates, meta], axis=1), blank], axis=0)
    chosen = (owner[:, None, None] == jnp.arange(twin_count, dtype=jnp.int32)[None, :, None]) & (
        slot[:, None, None] == jnp.arange(slot_count, dtype=jnp.int32)[None, None, :]
    )
    pick = jnp.where(jnp.any(chosen, axis=0), jnp.argmax(chosen, axis=0), pair_total)
    outgoing = jnp.take(tagged, pick.reshape(twin_count * slot_count), axis=0, mode="clip")
    outgoing = outgoing.reshape(twin_count, slot_count * (channels + meta_rows), samples)
    arrived = lax.all_to_all(outgoing, "twin", split_axis=0, concat_axis=0, tiled=True)
    arrived = arrived.reshape(twin_count, slot_count, channels + meta_rows, samples)

    arrived_rounds = arrived[:, :, channels, 0].astype(jnp.int32)
    hit = (arrived_rounds[:, :, None] == jnp.arange(rounds, dtype=jnp.int32)[None, None, :]).astype(jnp.bfloat16)

    def cleaned_rows(lo, hi):
        noise = jnp.einsum(
            "nsr,nscq->crq", hit, arrived[:, :, lo:hi], preferred_element_type=jnp.float32
        )
        return (record[lo:hi].astype(jnp.float32) - noise).astype(jnp.bfloat16)

    count = lax.axis_size("rcv")
    forward = [(i, i + 1) for i in range(count - 1)]
    backward = [(target, source) for source, target in forward]
    low = lax.ppermute(cleaned_rows(channels - 1, channels), "rcv", forward)
    high = lax.ppermute(cleaned_rows(0, 1), "rcv", backward)
    cleaned = cleaned_rows(0, channels)
    widened = jnp.concatenate([low, cleaned, high], axis=0).astype(jnp.float32)
    smooth = 0.5 * widened[1:-1] + 0.25 * (widened[:-2] + widened[2:])
    return smooth.astype(jnp.bfloat16)


def solution(mesh):
    placed = (P("rcv", None, "twin"), P("twin"), P("twin", None), P())
    return jax.shard_map(
        local, mesh=mesh, in_specs=placed, out_specs=P("rcv", None, "twin"), check_vma=False
    )
```

time: 214 us -> 159 us (0.74)
  blocking collectives: 149 us -> 105 us
  starting transfers between devices: 18.1 us -> 9.14 us
    unnamed x1 -> x0, blocking collectives: 149 us -> none
    all_to_all x0 -> x1, blocking collectives: none -> 105 us  [local(): lax.all_to_all(outgoing, 'twin', split_axis=0, concat_axis=0, tiled=True)]
    convert_element_type x1 -> x0, local copies, waits for them, and re-layouts: 18.5 us -> none  [local(): outgoing = jnp.einsum('kns,kcq->nscq', chosen.astype(jnp.bfloat16), estim...]
    slice x2 -> x3, local copies, waits for them, and re-layouts: 0.08 us -> 7.62 us  [the longest x2 7.61 us: cleaned_rows(): arrived[:, :, lo:hi]]
    gather x1 -> x2, local copies, waits for them, and re-layouts: 4.97 us -> 12.2 us  [the longest x1 7.28 us: local(): jnp.take(tagged, pick.reshape(twin_count * slot_count), axis=0, mode='clip')]
    all_to_all x1 -> x0, starting transfers between devices: 7.03 us -> none  [local(): lax.all_to_all(outgoing, 'twin', split_axis=0, concat_axis=0, tiled=True)]
    unnamed x10 -> x5, local copies, waits for them, and re-layouts: 0.6 us -> 3.38 us
    concatenate x0 -> x1, other arithmetic: none -> 2.3 us  [local(): jnp.concatenate([estimates, meta], axis=1)]
  transfers between devices with their start and end apart: 3 -> 2, of which waited for: 1 -> 0; matrix products, arithmetic and copies ran while one was open for 1% -> 6% of each run, Pallas kernels for 0% -> 0%
where the time goes in v2:
time: 159 us
  blocking collectives  105 us (66%)
  local copies, waits for them, and re-layouts  23.8 us (15%)
  matrix products  12.9 us (8%)
  starting transfers between devices  9.14 us (6%)
  other arithmetic  7.94 us (5%)
    all_to_all x1, blocking collectives, local(): lax.all_to_all(outgoing, 'twin', split_axis=0, concat_axis=0, tiled=True)  105 us
    dot_general x3, matrix products, cleaned_rows(): jnp.einsum('nsr,nscq->crq', hit, arrived[:, :, lo:hi], preferred_element_...  10.6 us
    slice x2, local copies, waits for them, and re-layouts, cleaned_rows(): arrived[:, :, lo:hi]  7.61 us
    gather x1, local copies, waits for them, and re-layouts, local(): jnp.take(tagged, pick.reshape(twin_count * slot_count), axis=0, mode='clip')  7.28 us
    gather x1, local copies, waits for them, and re-layouts, local(): guides = jnp.take(record, slip_block // twin_count, axis=1, mode='clip')  4.89 us
    ppermute x1, starting transfers between devices, local(): low = lax.ppermute(cleaned_rows(channels - 1, channels), 'rcv', forward)  4.84 us
    ppermute x1, starting transfers between devices, local(): high = lax.ppermute(cleaned_rows(0, 1), 'rcv', backward)  4.31 us
    unnamed x5, local copies, waits for them, and re-layouts  3.38 us
  transfers between devices with their start and end apart: 2, of which 0 were waited for; matrix products, arithmetic and copies ran while one was open for 6% of the time, Pallas kernels for 0%

profile of v2, /device:TPU:97, one launch (start us, length us, event | category | flops | bytes accessed | tf_op | source)
XLA Modules:
  0.0 158.6 jit_solution(12618826100498060467)
XLA Ops:
  0.0 0.8 and_select_fusion.2
  0.8 0.8 subtract_compare_fusion
  1.6 0.8 fusion.24
  2.3 0.1 ge.19
  2.4 0.1 ne.70
  2.5 0.1 rem.46
  2.6 0.1 div.28
  2.7 0.2 convert_reduce_fusion
  2.9 0.1 iota_compare_fusion.5
  3.0 0.1 and_reduce_fusion.1
  3.0 0.6 and_reduce_fusion
  3.7 0.1 copy.18
  3.7 0.1 reshape.160
  3.9 4.9 %gather_fusion = bf16[4,256,512]{2,0,1:T(4,128)(2,1)S(1)} fusion(bf16[256,8,512]{2,1,0:T(8,128)(2,1)} %param.4, s32[1024]{0:T(1024)S(1)} %pad_clamp_fusion.1), kind=kCustom, calls=%fused_computation | custom fusion | bytes 2097168 | tf_op jit(solution)/shard_map/jit(_take)/gather | solution.py:28
  8.8 2.3 %convolution_convert_fusion = bf16[256,4,4,512]{3,0,2,1:T(8,128)(2,1)S(1)} fusion(bf16[4,512,512]{2,1,0:T(8,128)(2,1)S(1)} %copy-done, bf16[256,4,512,1]{2,1,0,3:T(4,128)(2,1)S(1)} %bitcast.53), kind=kOutput, calls=%fused_computation.15 | convolution fusion | flops 2149580800 | bytes 7340032 | tf_op jit(solution)/shard_map/crp,hpq->rhcq/dot_general | solution.py:29
  11.1 0.1 broadcast_in_dim.15
  11.2 2.3 %fusion.4 = bf16[17,264,512]{2,1,0:T(8,128)(2,1)} fusion(bf16[16,8,512]{2,1,0:T(8,128)(2,1)S(1)} %broadcast_in_dim.15, bf16[16,256,512]{2,1,0:T(8,128)(2,1)S(1)} %bitcast.52), kind=kLoop, calls=%fused_computation.7 | loop fusion | flops 16084992 | bytes 8921088 | tf_op jit(solution)/shard_map/concatenate | solution.py:38
  13.5 7.3 %gather_fusion.1 = bf16[32,264,512]{2,1,0:T(8,128)(2,1)} fusion(bf16[17,264,512]{2,1,0:T(8,128)(2,1)} %fusion.4, s32[1024]{0:T(1024)S(1)} %pad_clamp_fusion), kind=kCustom, calls=%fused_computation.1 | custom fusion | bytes 17301632 | tf_op jit(solution)/shard_map/jit(_take)/gather | solution.py:43
  20.8 104.7 %all_to_all.5 = bf16[16,528,512]{2,1,0:T(8,128)(2,1)S(1)} all-to-all(bf16[16,528,512]{2,1,0:T(8,128)(2,1)} %bitcast.48), channel_id=1, replica_groups=mesh['rcv'=16,'twin'=16] {'twin'}, dimensions={0} | all-to-all | bytes 17301504 | tf_op jit(solution)/shard_map/all_to_all | solution.py:45
  125.5 3.3 %copy-done.1 = bf16[16,528,512]{2,1,0:T(8,128)(2,1)} copy-done((bf16[16,528,512]{2,1,0:T(8,128)(2,1)}, bf16[16,528,512]{2,1,0:T(8,128)(2,1)S(1)}, u32[]{:S(2)}) %copy-start.1) | copy-done | bytes 8650776
  128.8 0.1 fusion.27
  128.9 7.5 %slice.42 = bf16[16,2,256,512]{3,2,1,0:T(8,128)(2,1)} slice(bf16[16,2,264,512]{3,2,1,0:T(8,128)(2,1)} %bitcast.51), slice={[0:16], [0:2], [0:256], [0:512]} | slice | bytes 16777216 | tf_op jit(solution)/shard_map/slice | solution.py:53
  136.4 0.1 copy.28
  136.5 0.9 fusion.14
  137.4 0.9 fusion.15
  138.3 4.3 %collective-permute-start.1 = (bf16[1,8,512]{2,1,0:T(8,128)(2,1)S(1)}, bf16[1,8,512]{2,1,0:T(8,128)(2,1)S(1)}, u32[]{:S(2)}, u32[]{:S(2)}) collective-permute-start(bf16[1,8,512]{2,1,0:T(8,128)(2,1)S(1)} %fusion.15), channel_id=1, source_target_pairs={{16,0},{32,16},{48,32},{64,48},{80,64},{96,80},{112,96},{128,112},... | collective-permute-start | bytes 24584 | tf_op jit(solution)/shard_map/ppermute | solution.py:61
  142.6 4.8 %collective-permute-start = (bf16[1,8,512]{2,1,0:T(8,128)(2,1)S(1)}, bf16[1,8,512]{2,1,0:T(8,128)(2,1)S(1)}, u32[]{:S(2)}, u32[]{:S(2)}) collective-permute-start(bf16[1,8,512]{2,1,0:T(8,128)(2,1)S(1)} %fusion.14), channel_id=1, source_target_pairs={{0,16},{16,32},{32,48},{48,64},{64,80},{80,96},{96,112},{112,128},... | collective-permute-start | bytes 24584 | tf_op jit(solution)/shard_map/ppermute | solution.py:60
  147.5 8.8 %fusion.8 = bf16[256,8,512]{2,1,0:T(8,128)(2,1)S(1)} fusion(bf16[256,8,512]{2,1,0:T(8,128)(2,1)} %param.4, bf16[16,2,256,512]{3,2,1,0:T(8,128)(2,1)} %slice.42, s32[16,2]{0,1:T(2,128)S(1)} %bitcast_convert_fusion), kind=kOutput, calls=%fused_computation.14 | convolution fusion | flops 70254848 | bytes 12583040 | tf_op jit(solution)/shard_map/nsr,nscq->crq/dot_general | solution.py:52
  156.3 0.0 collective-permute-done.1
  156.3 0.0 collective-permute-done
  156.3 0.3 maximum_convert_fusion
  156.6 2.0 %fusion.7 = bf16[256,8,512]{2,1,0:T(8,128)(2,1)} fusion(f32[258,8,512]{2,1,0:T(8,128)S(1)} %maximum_convert_fusion), kind=kLoop, calls=%fused_computation.11 | loop fusion | flops 5242880 | bytes 14680064 | tf_op jit(solution)/shard_map/convert_element_type | solution.py:65
  (10 shorter events, 0.1 us)
Async XLA Ops:
  0.0 8.7 %copy-start = (bf16[4,512,512]{2,1,0:T(8,128)(2,1)S(1)}, bf16[4,512,512]{2,1,0:T(8,128)(2,1)}, u32[]{:S(2)}) copy-start(bf16[4,512,512]{2,1,0:T(8,128)(2,1)} %param.7) | copy-start | bytes 6291460
  125.5 3.3 %copy-start.1 = (bf16[16,528,512]{2,1,0:T(8,128)(2,1)}, bf16[16,528,512]{2,1,0:T(8,128)(2,1)S(1)}, u32[]{:S(2)}) copy-start(bf16[16,528,512]{2,1,0:T(8,128)(2,1)S(1)} %all_to_all.5) | copy-start | bytes 25952260
  138.3 18.0 %collective-permute-start.1 = (bf16[1,8,512]{2,1,0:T(8,128)(2,1)S(1)}, bf16[1,8,512]{2,1,0:T(8,128)(2,1)S(1)}, u32[]{:S(2)}, u32[]{:S(2)}) collective-permute-start(bf16[1,8,512]{2,1,0:T(8,128)(2,1)S(1)} %fusion.15), channel_id=1, source_target_pairs={{16,0},{32,16},{48,32},{64,48},{80,64},{96,80},{112,96},{128,112},... | collective-permute-start | bytes 24584 | tf_op jit(solution)/shard_map/ppermute | solution.py:61
  142.6 13.7 %collective-permute-start = (bf16[1,8,512]{2,1,0:T(8,128)(2,1)S(1)}, bf16[1,8,512]{2,1,0:T(8,128)(2,1)S(1)}, u32[]{:S(2)}, u32[]{:S(2)}) collective-permute-start(bf16[1,8,512]{2,1,0:T(8,128)(2,1)S(1)} %fusion.14), channel_id=1, source_target_pairs={{0,16},{16,32},{32,48},{48,64},{64,80},{80,96},{96,112},{112,128},... | collective-permute-start | bytes 24584 | tf_op jit(solution)/shard_map/ppermute | solution.py:60

commit v3 on v2

--- a/solution.py
+++ b/solution.py
@@ -48,11 +48,10 @@
     arrived_rounds = arrived[:, :, channels, 0].astype(jnp.int32)
     hit = (arrived_rounds[:, :, None] == jnp.arange(rounds, dtype=jnp.int32)[None, None, :]).astype(jnp.bfloat16)
 
+    noise = jnp.einsum("nsr,nscq->crq", hit, arrived, preferred_element_type=jnp.float32)
+
     def cleaned_rows(lo, hi):
-        noise = jnp.einsum(
-            "nsr,nscq->crq", hit, arrived[:, :, lo:hi], preferred_element_type=jnp.float32
-        )
-        return (record[lo:hi].astype(jnp.float32) - noise).astype(jnp.bfloat16)
+        return (record[lo:hi].astype(jnp.float32) - noise[lo:hi]).astype(jnp.bfloat16)
 
     count = lax.axis_size("rcv")
     forward = [(i, i + 1) for i in range(count - 1)]

time: 159 us -> 154 us (0.969)
  local copies, waits for them, and re-layouts: 23.8 us -> 16.5 us
  waiting for transfers between devices: 0.01 us -> 3.45 us
  matrix products: 12.9 us -> 10.7 us
    slice x2 -> x0, local copies, waits for them, and re-layouts: 7.61 us -> none  [cleaned_rows(): arrived[:, :, lo:hi]]
    ppermute x1, waiting for transfers between devices: 0.01 us -> 3.45 us  [local(): high = lax.ppermute(cleaned_rows(0, 1), 'rcv', backward)]
    ppermute x1, starting transfers between devices: 4.31 us -> 1.92 us  [local(): high = lax.ppermute(cleaned_rows(0, 1), 'rcv', backward)]
    dot_general x3 -> x1, matrix products: 10.6 us -> 8.36 us  [local(): jnp.einsum('nsr,nscq->crq', hit, arrived, preferred_element_type=jnp.floa...]
    ppermute x1, starting transfers between devices: 4.84 us -> 7.04 us  [local(): low = lax.ppermute(cleaned_rows(channels - 1, channels), 'rcv', forward)]
    unnamed x5 -> x7, local copies, waits for them, and re-layouts: 3.38 us -> 3.4 us
  transfers between devices with their start and end apart: 2 -> 2, of which waited for: 0 -> 1; matrix products, arithmetic and copies ran while one was open for 6% -> 1% of each run, Pallas kernels for 0% -> 0%
where the time goes in v3:
time: 154 us; the launch traced here: 153 us
  blocking collectives  105 us (68%)
  local copies, waits for them, and re-layouts  16.5 us (11%)
  matrix products  10.7 us (7%)
  starting transfers between devices  8.96 us (6%)
  other arithmetic  8.73 us (6%)
  waiting for transfers between devices  3.45 us (2%)
    all_to_all x1, blocking collectives, local(): lax.all_to_all(outgoing, 'twin', split_axis=0, concat_axis=0, tiled=True)  105 us
    dot_general x1, matrix products, local(): jnp.einsum('nsr,nscq->crq', hit, arrived, preferred_element_type=jnp.floa...  8.36 us
    gather x1, local copies, waits for them, and re-layouts, local(): jnp.take(tagged, pick.reshape(twin_count * slot_count), axis=0, mode='clip')  7.28 us
    ppermute x1, starting transfers between devices, local(): low = lax.ppermute(cleaned_rows(channels - 1, channels), 'rcv', forward)  7.04 us
    gather x1, local copies, waits for them, and re-layouts, local(): guides = jnp.take(record, slip_block // twin_count, axis=1, mode='clip')  5.2 us
    ppermute x1, waiting for transfers between devices, local(): high = lax.ppermute(cleaned_rows(0, 1), 'rcv', backward)  3.45 us
    unnamed x7, local copies, waits for them, and re-layouts  3.4 us
  transfers between devices with their start and end apart: 2, of which 1 were waited for; matrix products, arithmetic and copies ran while one was open for 1% of the time, Pallas kernels for 0%

profile of v3, /device:TPU:97, one launch (start us, length us, event | category | flops | bytes accessed | tf_op | source)
XLA Modules:
  0.0 153.4 jit_solution(6305830289966880282)
XLA Ops:
  0.0 0.0 copy-start
  0.0 0.8 and_select_fusion.2
  0.8 0.8 subtract_compare_fusion
  1.6 0.8 fusion.21
  2.3 0.1 ge.19
  2.4 0.1 ne.70
  2.5 0.1 rem.46
  2.6 0.1 div.28
  2.7 0.2 convert_reduce_fusion
  2.9 0.1 iota_compare_fusion.3
  3.0 0.1 and_reduce_fusion.1
  3.0 0.6 and_reduce_fusion
  3.7 0.1 copy.14
  3.7 0.1 reshape.150
  3.9 5.2 %gather_fusion = bf16[4,256,512]{2,0,1:T(4,128)(2,1)S(1)} fusion(bf16[256,8,512]{2,1,0:T(8,128)(2,1)} %param.4, s32[1024]{0:T(1024)S(1)} %pad_clamp_fusion.1), kind=kCustom, calls=%fused_computation | custom fusion | bytes 2097168 | tf_op jit(solution)/shard_map/jit(_take)/gather | solution.py:28
  9.1 0.0 copy-done
  9.1 2.3 %convolution_convert_fusion = bf16[256,4,4,512]{3,0,2,1:T(8,128)(2,1)S(1)} fusion(bf16[4,512,512]{2,1,0:T(8,128)(2,1)S(1)} %copy-done, bf16[256,4,512,1]{2,1,0,3:T(4,128)(2,1)S(1)} %bitcast.26), kind=kOutput, calls=%fused_computation.15 | convolution fusion | flops 2149580800 | bytes 7340032 | tf_op jit(solution)/shard_map/crp,hpq->rhcq/dot_general | solution.py:29
  11.4 0.1 broadcast_in_dim.15
  11.5 2.3 %fusion.4 = bf16[17,264,512]{2,1,0:T(8,128)(2,1)} fusion(bf16[16,8,512]{2,1,0:T(8,128)(2,1)S(1)} %broadcast_in_dim.15, bf16[16,256,512]{2,1,0:T(8,128)(2,1)S(1)} %bitcast.25), kind=kLoop, calls=%fused_computation.7 | loop fusion | flops 16084992 | bytes 8921088 | tf_op jit(solution)/shard_map/concatenate | solution.py:38
  13.8 7.3 %gather_fusion.1 = bf16[32,264,512]{2,1,0:T(8,128)(2,1)} fusion(bf16[17,264,512]{2,1,0:T(8,128)(2,1)} %fusion.4, s32[1024]{0:T(1024)S(1)} %pad_clamp_fusion), kind=kCustom, calls=%fused_computation.1 | custom fusion | bytes 17301632 | tf_op jit(solution)/shard_map/jit(_take)/gather | solution.py:43
  21.1 105.0 %all_to_all.5 = bf16[16,528,512]{2,1,0:T(8,128)(2,1)S(1)} all-to-all(bf16[16,528,512]{2,1,0:T(8,128)(2,1)} %bitcast.24), channel_id=1, replica_groups=mesh['rcv'=16,'twin'=16] {'twin'}, dimensions={0} | all-to-all | bytes 17301504 | tf_op jit(solution)/shard_map/all_to_all | solution.py:45
  126.1 3.3 %copy-done.2 = bf16[16,528,512]{2,1,0:T(8,128)(2,1)} copy-done((bf16[16,528,512]{2,1,0:T(8,128)(2,1)}, bf16[16,528,512]{2,1,0:T(8,128)(2,1)S(1)}, u32[]{:S(2)}) %copy-start.2) | copy-done | bytes 8650776
  129.4 0.1 copy.21
  129.5 8.4 %fusion.9 = f32[264,8,512]{2,1,0:T(8,128)S(1)} fusion(bf16[16,2,264,512]{3,2,1,0:T(8,128)(2,1)} %bitcast.23, s32[16,2]{0,1:T(2,128)S(1)} %bitcast_convert_fusion), kind=kOutput, calls=%fused_computation.16 | convolution fusion | flops 69206272 | bytes 12976256 | tf_op jit(solution)/shard_map/nsr,nscq->crq/dot_general | solution.py:51
  137.9 0.0 copy-done.1
  137.9 7.0 %collective-permute-start = (bf16[1,8,512]{2,1,0:T(8,128)(2,1)S(1)}, bf16[1,8,512]{2,1,0:T(8,128)(2,1)S(1)}, u32[]{:S(2)}, u32[]{:S(2)}) collective-permute-start(bf16[1,8,512]{2,1,0:T(8,128)(2,1)S(1)} %get-tuple-element.7), channel_id=1, source_target_pairs={{0,16},{16,32},{32,48},{48,64},{64,80},{80,96},{96,112},{112,128},... | collective-permute-start | bytes 24584 | tf_op jit(solution)/shard_map/ppermute | solution.py:59
  144.9 1.9 %collective-permute-start.1 = (bf16[1,8,512]{2,1,0:T(8,128)(2,1)S(1)}, bf16[1,8,512]{2,1,0:T(8,128)(2,1)S(1)}, u32[]{:S(2)}, u32[]{:S(2)}) collective-permute-start(bf16[1,8,512]{2,1,0:T(8,128)(2,1)S(1)} %get-tuple-element.8), channel_id=1, source_target_pairs={{16,0},{32,16},{48,32},{64,48},{80,64},{96,80},{112,96},{128,112},... | collective-permute-start | bytes 24584 | tf_op jit(solution)/shard_map/ppermute | solution.py:60
  146.9 0.8 fusion.8
  147.6 0.0 collective-permute-done
  147.7 3.4 %collective-permute-done.1 = bf16[1,8,512]{2,1,0:T(8,128)(2,1)S(1)} collective-permute-done((bf16[1,8,512]{2,1,0:T(8,128)(2,1)S(1)}, bf16[1,8,512]{2,1,0:T(8,128)(2,1)S(1)}, u32[]{:S(2)}, u32[]{:S(2)}) %collective-permute-start.1) | collective-permute-done | bytes 8224 | tf_op jit(solution)/shard_map/ppermute | solution.py:60
  151.1 0.3 maximum_convert_fusion
  151.4 2.0 %fusion.7 = bf16[256,8,512]{2,1,0:T(8,128)(2,1)} fusion(f32[258,8,512]{2,1,0:T(8,128)S(1)} %maximum_convert_fusion), kind=kLoop, calls=%fused_computation.11 | loop fusion | flops 5242880 | bytes 14680064 | tf_op jit(solution)/shard_map/convert_element_type | solution.py:64
  (10 shorter events, 0.1 us)
Async XLA Ops:
  0.0 9.1 %copy-start = (bf16[4,512,512]{2,1,0:T(8,128)(2,1)S(1)}, bf16[4,512,512]{2,1,0:T(8,128)(2,1)}, u32[]{:S(2)}) copy-start(bf16[4,512,512]{2,1,0:T(8,128)(2,1)} %param.7) | copy-start | bytes 6291460
  126.1 3.3 %copy-start.2 = (bf16[16,528,512]{2,1,0:T(8,128)(2,1)}, bf16[16,528,512]{2,1,0:T(8,128)(2,1)S(1)}, u32[]{:S(2)}) copy-start(bf16[16,528,512]{2,1,0:T(8,128)(2,1)S(1)} %all_to_all.5) | copy-start | bytes 25952260
  129.5 8.4 %copy-start.1 = (bf16[256,8,512]{2,1,0:T(8,128)(2,1)S(1)}, bf16[256,8,512]{2,1,0:T(8,128)(2,1)}, u32[]{:S(2)}) copy-start(bf16[256,8,512]{2,1,0:T(8,128)(2,1)} %param.4) | copy-start | bytes 6291460
  137.9 9.8 %collective-permute-start = (bf16[1,8,512]{2,1,0:T(8,128)(2,1)S(1)}, bf16[1,8,512]{2,1,0:T(8,128)(2,1)S(1)}, u32[]{:S(2)}, u32[]{:S(2)}) collective-permute-start(bf16[1,8,512]{2,1,0:T(8,128)(2,1)S(1)} %get-tuple-element.7), channel_id=1, source_target_pairs={{0,16},{16,32},{32,48},{48,64},{64,80},{80,96},{96,112},{112,128},... | collective-permute-start | bytes 24584 | tf_op jit(solution)/shard_map/ppermute | solution.py:59
  144.9 6.2 %collective-permute-start.1 = (bf16[1,8,512]{2,1,0:T(8,128)(2,1)S(1)}, bf16[1,8,512]{2,1,0:T(8,128)(2,1)S(1)}, u32[]{:S(2)}, u32[]{:S(2)}) collective-permute-start(bf16[1,8,512]{2,1,0:T(8,128)(2,1)S(1)} %get-tuple-element.8), channel_id=1, source_target_pairs={{16,0},{32,16},{48,32},{64,48},{80,64},{96,80},{112,96},{128,112},... | collective-permute-start | bytes 24584 | tf_op jit(solution)/shard_map/ppermute | solution.py:60

commit v4 on v3

--- a/solution.py
+++ b/solution.py
@@ -25,9 +25,11 @@
     pair_total = rec_count * order_count
     slot_count = pair_total // twin_count + 1
 
-    guides = jnp.take(record, slip_block // twin_count, axis=1, mode="clip")
+    planes = jnp.transpose(record, (1, 0, 2))
+
+    guides = jnp.take(planes, slip_block // twin_count, axis=0, mode="clip")
     estimates = jnp.einsum(
-        "crp,hpq->rhcq", guides, order_ops, preferred_element_type=jnp.float32
+        "rcp,hpq->rhcq", guides, order_ops, preferred_element_type=jnp.float32
     ).astype(jnp.bfloat16)
     estimates = estimates.reshape(pair_total, channels, samples)
 
@@ -47,11 +49,10 @@
 
     arrived_rounds = arrived[:, :, channels, 0].astype(jnp.int32)
     hit = (arrived_rounds[:, :, None] == jnp.arange(rounds, dtype=jnp.int32)[None, None, :]).astype(jnp.bfloat16)
-
-    noise = jnp.einsum("nsr,nscq->crq", hit, arrived, preferred_element_type=jnp.float32)
+    noise = jnp.einsum("nsr,nscq->rcq", hit, arrived, preferred_element_type=jnp.float32)
 
     def cleaned_rows(lo, hi):
-        return (record[lo:hi].astype(jnp.float32) - noise[lo:hi]).astype(jnp.bfloat16)
+        return (planes[:, lo:hi].astype(jnp.float32) - noise[:, lo:hi]).astype(jnp.bfloat16)
 
     count = lax.axis_size("rcv")
     forward = [(i, i + 1) for i in range(count - 1)]
@@ -59,9 +60,9 @@
     low = lax.ppermute(cleaned_rows(channels - 1, channels), "rcv", forward)
     high = lax.ppermute(cleaned_rows(0, 1), "rcv", backward)
     cleaned = cleaned_rows(0, channels)
-    widened = jnp.concatenate([low, cleaned, high], axis=0).astype(jnp.float32)
-    smooth = 0.5 * widened[1:-1] + 0.25 * (widened[:-2] + widened[2:])
-    return smooth.astype(jnp.bfloat16)
+    widened = jnp.concatenate([low, cleaned, high], axis=1).astype(jnp.float32)
+    smooth = 0.5 * widened[:, 1:-1] + 0.25 * (widened[:, :-2] + widened[:, 2:])
+    return jnp.transpose(smooth.astype(jnp.bfloat16), (1, 0, 2))
 
 
 def solution(mesh):

time: 154 us -> 154 us (level)
    transpose x0 -> x1, local copies, waits for them, and re-layouts: none -> 3.58 us  [local(): planes = jnp.transpose(record, (1, 0, 2))]
    gather x1, local copies, waits for them, and re-layouts: 5.2 us -> 2.2 us  [local(): guides = jnp.take(planes, slip_block // twin_count, axis=0, mode='clip')]
    convert_element_type x4 -> x3, other arithmetic: 3.11 us -> 1.12 us  [the longest x2 0.79 us: cleaned_rows(): (planes[:, lo:hi].astype(jnp.float32) - noise[:, lo:hi]).astype(jnp.bfloa...]
    transpose x0 -> x1, other arithmetic: none -> 1.99 us  [local(): return jnp.transpose(smooth.astype(jnp.bfloat16), (1, 0, 2))]
where the time goes in v4:
time: 154 us
  blocking collectives  105 us (68%)
  local copies, waits for them, and re-layouts  17.1 us (11%)
  matrix products  10.7 us (7%)
  starting transfers between devices  9 us (6%)
  other arithmetic  8.73 us (6%)
  waiting for transfers between devices  3.45 us (2%)
    all_to_all x1, blocking collectives, local(): lax.all_to_all(outgoing, 'twin', split_axis=0, concat_axis=0, tiled=True)  105 us
    dot_general x1, matrix products, local(): jnp.einsum('nsr,nscq->rcq', hit, arrived, preferred_element_type=jnp.floa...  8.37 us
    gather x1, local copies, waits for them, and re-layouts, local(): jnp.take(tagged, pick.reshape(twin_count * slot_count), axis=0, mode='clip')  7.3 us
    ppermute x1, starting transfers between devices, local(): low = lax.ppermute(cleaned_rows(channels - 1, channels), 'rcv', forward)  7.08 us
    transpose x1, local copies, waits for them, and re-layouts, local(): planes = jnp.transpose(record, (1, 0, 2))  3.58 us
    ppermute x1, waiting for transfers between devices, local(): high = lax.ppermute(cleaned_rows(0, 1), 'rcv', backward)  3.45 us
    unnamed x7, local copies, waits for them, and re-layouts  3.4 us
  transfers between devices with their start and end apart: 2, of which 1 were waited for; matrix products, arithmetic and copies ran while one was open for 1% of the time, Pallas kernels for 0%

profile of v4, /device:TPU:97, one launch (start us, length us, event | category | flops | bytes accessed | tf_op | source)
XLA Modules:
  0.0 153.9 jit_solution(5295985463804763642)
XLA Ops:
  0.0 0.0 copy-start
  0.0 0.8 and_select_fusion.2
  0.8 0.8 subtract_compare_fusion
  1.6 0.8 fusion.22
  2.3 0.1 ge.19
  2.4 0.1 ne.70
  2.5 0.1 rem.46
  2.6 0.1 div.28
  2.7 0.2 convert_reduce_fusion
  2.9 0.1 iota_compare_fusion.3
  3.0 0.1 and_reduce_fusion.1
  3.0 0.6 and_reduce_fusion
  3.7 0.1 copy.14
  3.7 0.1 reshape.150
  3.9 3.6 %copy.13 = bf16[8,256,512]{2,1,0:T(8,128)(2,1)} copy(bf16[8,256,512]{2,0,1:T(8,128)(2,1)} %bitcast.29) | data formatting | bytes 4194304 | tf_op jit(solution)/shard_map/transpose | solution.py:28
  7.4 2.2 %gather_fusion = bf16[4,256,512]{2,1,0:T(8,128)(2,1)S(1)} fusion(bf16[8,256,512]{2,1,0:T(8,128)(2,1)} %copy.13, s32[1024]{0:T(1024)S(1)} %pad_clamp_fusion.1), kind=kCustom, calls=%fused_computation | custom fusion | bytes 2097168 | tf_op jit(solution)/shard_map/jit(_take)/gather | solution.py:30
  9.7 2.3 %convolution_convert_fusion = bf16[4,256,4,512]{3,1,2,0:T(8,128)(2,1)S(1)} fusion(bf16[4,512,512]{2,1,0:T(8,128)(2,1)S(1)} %copy-done, bf16[4,256,512]{2,1,0:T(8,128)(2,1)S(1)} %gather_fusion), kind=kOutput, calls=%fused_computation.15 | convolution fusion | flops 2149580800 | bytes 7340032 | tf_op jit(solution)/shard_map/rcp,hpq->rhcq/dot_general | solution.py:31
  12.0 0.1 broadcast_in_dim.15
  12.1 2.3 %fusion.4 = bf16[17,264,512]{2,1,0:T(8,128)(2,1)} fusion(bf16[16,8,512]{2,1,0:T(8,128)(2,1)S(1)} %broadcast_in_dim.15, bf16[16,256,512]{2,1,0:T(8,128)(2,1)S(1)} %bitcast.31), kind=kLoop, calls=%fused_computation.7 | loop fusion | flops 16084992 | bytes 8921088 | tf_op jit(solution)/shard_map/concatenate | solution.py:40
  14.4 7.3 %gather_fusion.1 = bf16[32,264,512]{2,1,0:T(8,128)(2,1)} fusion(bf16[17,264,512]{2,1,0:T(8,128)(2,1)} %fusion.4, s32[1024]{0:T(1024)S(1)} %pad_clamp_fusion), kind=kCustom, calls=%fused_computation.1 | custom fusion | bytes 17301632 | tf_op jit(solution)/shard_map/jit(_take)/gather | solution.py:45
  21.7 104.8 %all_to_all.5 = bf16[16,528,512]{2,1,0:T(8,128)(2,1)S(1)} all-to-all(bf16[16,528,512]{2,1,0:T(8,128)(2,1)} %bitcast.28), channel_id=1, replica_groups=mesh['rcv'=16,'twin'=16] {'twin'}, dimensions={0} | all-to-all | bytes 17301504 | tf_op jit(solution)/shard_map/all_to_all | solution.py:47
  126.5 3.3 %copy-done.1 = bf16[16,528,512]{2,1,0:T(8,128)(2,1)} copy-done((bf16[16,528,512]{2,1,0:T(8,128)(2,1)}, bf16[16,528,512]{2,1,0:T(8,128)(2,1)S(1)}, u32[]{:S(2)}) %copy-start.1) | copy-done | bytes 8650776
  129.8 0.1 copy.19
  129.9 8.4 %fusion.9 = f32[8,264,512]{2,0,1:T(8,128)S(1)} fusion(bf16[16,2,264,512]{3,2,1,0:T(8,128)(2,1)} %bitcast.27, s32[16,2]{0,1:T(2,128)S(1)} %bitcast_convert_fusion), kind=kOutput, calls=%fused_computation.16 | convolution fusion | flops 69206272 | bytes 12976256 | tf_op jit(solution)/shard_map/nsr,nscq->rcq/dot_general | solution.py:52
  138.3 0.0 copy-done.2
  138.3 7.1 %collective-permute-start = (bf16[8,1,512]{2,0,1:T(8,128)(2,1)S(1)}, bf16[8,1,512]{2,0,1:T(8,128)(2,1)S(1)}, u32[]{:S(2)}, u32[]{:S(2)}) collective-permute-start(bf16[8,1,512]{2,0,1:T(8,128)(2,1)S(1)} %get-tuple-element.7), channel_id=1, source_target_pairs={{0,16},{16,32},{32,48},{48,64},{64,80},{80,96},{96,112},{112,128},... | collective-permute-start | bytes 24584 | tf_op jit(solution)/shard_map/ppermute | solution.py:60
  145.4 1.9 %collective-permute-start.1 = (bf16[8,1,512]{2,0,1:T(8,128)(2,1)S(1)}, bf16[8,1,512]{2,0,1:T(8,128)(2,1)S(1)}, u32[]{:S(2)}, u32[]{:S(2)}) collective-permute-start(bf16[8,1,512]{2,0,1:T(8,128)(2,1)S(1)} %get-tuple-element.8), channel_id=1, source_target_pairs={{16,0},{32,16},{48,32},{64,48},{80,64},{96,80},{112,96},{128,112},... | collective-permute-start | bytes 24584 | tf_op jit(solution)/shard_map/ppermute | solution.py:61
  147.3 0.8 fusion.8
  148.1 0.0 collective-permute-done
  148.1 3.4 %collective-permute-done.1 = bf16[8,1,512]{2,0,1:T(8,128)(2,1)S(1)} collective-permute-done((bf16[8,1,512]{2,0,1:T(8,128)(2,1)S(1)}, bf16[8,1,512]{2,0,1:T(8,128)(2,1)S(1)}, u32[]{:S(2)}, u32[]{:S(2)}) %collective-permute-start.1) | collective-permute-done | bytes 8224 | tf_op jit(solution)/shard_map/ppermute | solution.py:61
  151.5 0.3 maximum_convert_fusion
  151.9 2.0 %fusion.12 = bf16[256,8,512]{2,1,0:T(8,128)(2,1)} fusion(f32[8,258,512]{2,0,1:T(8,128)S(1)} %maximum_convert_fusion), kind=kLoop, calls=%fused_computation.18 | loop fusion | flops 5242880 | bytes 14680064 | tf_op jit(solution)/shard_map/transpose | solution.py:65
  (11 shorter events, 0.1 us)
Async XLA Ops:
  0.0 9.6 %copy-start = (bf16[4,512,512]{2,1,0:T(8,128)(2,1)S(1)}, bf16[4,512,512]{2,1,0:T(8,128)(2,1)}, u32[]{:S(2)}) copy-start(bf16[4,512,512]{2,1,0:T(8,128)(2,1)} %param.7) | copy-start | bytes 6291460
  126.5 3.3 %copy-start.1 = (bf16[16,528,512]{2,1,0:T(8,128)(2,1)}, bf16[16,528,512]{2,1,0:T(8,128)(2,1)S(1)}, u32[]{:S(2)}) copy-start(bf16[16,528,512]{2,1,0:T(8,128)(2,1)S(1)} %all_to_all.5) | copy-start | bytes 25952260
  129.9 8.4 %copy-start.2 = (bf16[256,8,512]{2,1,0:T(8,128)(2,1)S(1)}, bf16[256,8,512]{2,1,0:T(8,128)(2,1)}, u32[]{:S(2)}) copy-start(bf16[256,8,512]{2,1,0:T(8,128)(2,1)} %param.4) | copy-start | bytes 6291460
  138.3 9.8 %collective-permute-start = (bf16[8,1,512]{2,0,1:T(8,128)(2,1)S(1)}, bf16[8,1,512]{2,0,1:T(8,128)(2,1)S(1)}, u32[]{:S(2)}, u32[]{:S(2)}) collective-permute-start(bf16[8,1,512]{2,0,1:T(8,128)(2,1)S(1)} %get-tuple-element.7), channel_id=1, source_target_pairs={{0,16},{16,32},{32,48},{48,64},{64,80},{80,96},{96,112},{112,128},... | collective-permute-start | bytes 24584 | tf_op jit(solution)/shard_map/ppermute | solution.py:60
  145.4 6.2 %collective-permute-start.1 = (bf16[8,1,512]{2,0,1:T(8,128)(2,1)S(1)}, bf16[8,1,512]{2,0,1:T(8,128)(2,1)S(1)}, u32[]{:S(2)}, u32[]{:S(2)}) collective-permute-start(bf16[8,1,512]{2,0,1:T(8,128)(2,1)S(1)} %get-tuple-element.8), channel_id=1, source_target_pairs={{16,0},{32,16},{48,32},{64,48},{80,64},{96,80},{112,96},{128,112},... | collective-permute-start | bytes 24584 | tf_op jit(solution)/shard_map/ppermute | solution.py:61

commit v5 on v3

--- a/solution.py
+++ b/solution.py
@@ -48,7 +48,14 @@
     arrived_rounds = arrived[:, :, channels, 0].astype(jnp.int32)
     hit = (arrived_rounds[:, :, None] == jnp.arange(rounds, dtype=jnp.int32)[None, None, :]).astype(jnp.bfloat16)
 
-    noise = jnp.einsum("nsr,nscq->crq", hit, arrived, preferred_element_type=jnp.float32)
+    sub = 8
+    blocks = (channels + meta_rows) // sub
+    spread = jnp.einsum(
+        "jr,ik->irjk", hit.reshape(twin_count * slot_count, rounds), jnp.eye(sub, dtype=jnp.bfloat16)
+    )
+    stacked = arrived.reshape(twin_count * slot_count, blocks, sub, samples)
+    noise = jnp.einsum("irjk,jbkq->birq", spread, stacked, preferred_element_type=jnp.float32)
+    noise = noise.reshape(blocks * sub, rounds, samples)
 
     def cleaned_rows(lo, hi):
         return (record[lo:hi].astype(jnp.float32) - noise[lo:hi]).astype(jnp.bfloat16)

time: 154 us -> 204 us (1.32)
  waiting for transfers between devices: 3.45 us -> 155 us
  blocking collectives: 105 us -> 0 us
  starting transfers between devices: 8.96 us -> 15.7 us
  matrix products: 10.7 us -> 6.99 us
    all_to_all x0 -> x1, waiting for transfers between devices: none -> 152 us  [local(): lax.all_to_all(outgoing, 'twin', split_axis=0, concat_axis=0, tiled=True)]
    all_to_all x1 -> x0, blocking collectives: 105 us -> none  [local(): lax.all_to_all(outgoing, 'twin', split_axis=0, concat_axis=0, tiled=True)]
    all_to_all x0 -> x1, starting transfers between devices: none -> 6.75 us  [local(): lax.all_to_all(outgoing, 'twin', split_axis=0, concat_axis=0, tiled=True)]
    dot_general x1, matrix products: 8.36 us -> 4.65 us  [local(): jnp.einsum('irjk,jbkq->birq', spread, stacked, preferred_element_type=jnp...]
    unnamed x7 -> x4, local copies, waits for them, and re-layouts: 3.4 us -> 1.13 us
  transfers between devices with their start and end apart: 2 -> 3, of which waited for: 1 -> 2; matrix products, arithmetic and copies ran while one was open for 1% -> 0% of each run, Pallas kernels for 0% -> 0%
where the time goes in v5:
time: 204 us; the launch traced here: 203 us
  waiting for transfers between devices  155 us (76%)
  starting transfers between devices  15.7 us (8%)
  local copies, waits for them, and re-layouts  14.5 us (7%)
  other arithmetic  10.3 us (5%)
  matrix products  6.99 us (3%)
    all_to_all x1, waiting for transfers between devices, local(): lax.all_to_all(outgoing, 'twin', split_axis=0, concat_axis=0, tiled=True)  152 us
    gather x1, local copies, waits for them, and re-layouts, local(): jnp.take(tagged, pick.reshape(twin_count * slot_count), axis=0, mode='clip')  7.28 us
    ppermute x1, starting transfers between devices, local(): low = lax.ppermute(cleaned_rows(channels - 1, channels), 'rcv', forward)  7.03 us
    all_to_all x1, starting transfers between devices, local(): lax.all_to_all(outgoing, 'twin', split_axis=0, concat_axis=0, tiled=True)  6.75 us
    gather x1, local copies, waits for them, and re-layouts, local(): guides = jnp.take(record, slip_block // twin_count, axis=1, mode='clip')  4.96 us
    dot_general x1, matrix products, local(): jnp.einsum('irjk,jbkq->birq', spread, stacked, preferred_element_type=jnp...  4.65 us
  transfers between devices with their start and end apart: 3, of which 2 were waited for; matrix products, arithmetic and copies ran while one was open for 0% of the time, Pallas kernels for 0%

profile of v5, /device:TPU:97, one launch (start us, length us, event | category | flops | bytes accessed | tf_op | source)
XLA Modules:
  0.0 202.7 jit_solution(10123796656459742464)
XLA Ops:
  0.0 0.9 fusion.22
  0.9 0.8 subtract_compare_fusion
  1.7 0.1 div.28
  1.8 0.1 rem.46
  1.8 0.1 ge.19
  1.9 0.1 ne.70
  2.0 0.1 iota_compare_fusion.3
  2.1 0.2 convert_reduce_fusion
  2.3 0.6 and_reduce_fusion
  2.9 0.1 and_reduce_fusion.1
  3.0 0.7 and_select_fusion.2
  3.7 0.1 copy.9
  3.7 0.1 reshape.158
  3.9 5.0 %gather_fusion = bf16[4,256,512]{2,0,1:T(4,128)(2,1)S(1)} fusion(bf16[256,8,512]{2,1,0:T(8,128)(2,1)} %param.4, s32[1024]{0:T(1024)S(1)} %pad_clamp_fusion.1), kind=kCustom, calls=%fused_computation | custom fusion | bytes 2097168 | tf_op jit(solution)/shard_map/jit(_take)/gather | solution.py:28
  8.8 2.3 %convolution_convert_fusion = bf16[256,4,4,512]{3,0,2,1:T(8,128)(2,1)S(1)} fusion(bf16[4,512,512]{2,1,0:T(8,128)(2,1)S(1)} %copy-done, bf16[256,4,512,1]{2,1,0,3:T(4,128)(2,1)S(1)} %bitcast.33), kind=kOutput, calls=%fused_computation.15 | convolution fusion | flops 2149580800 | bytes 7340032 | tf_op jit(solution)/shard_map/crp,hpq->rhcq/dot_general | solution.py:29
  11.2 0.1 broadcast_in_dim.15
  11.3 2.3 %fusion.4 = bf16[17,264,512]{2,1,0:T(8,128)(2,1)} fusion(bf16[16,8,512]{2,1,0:T(8,128)(2,1)S(1)} %broadcast_in_dim.15, bf16[16,256,512]{2,1,0:T(8,128)(2,1)S(1)} %bitcast.30), kind=kLoop, calls=%fused_computation.7 | loop fusion | flops 16084992 | bytes 8921088 | tf_op jit(solution)/shard_map/concatenate | solution.py:38
  13.6 7.3 %gather_fusion.1 = bf16[32,264,512]{2,1,0:T(8,128)(2,1)} fusion(bf16[17,264,512]{2,1,0:T(8,128)(2,1)} %fusion.4, s32[1024]{0:T(1024)S(1)} %pad_clamp_fusion), kind=kCustom, calls=%fused_computation.1 | custom fusion | bytes 17301632 | tf_op jit(solution)/shard_map/jit(_take)/gather | solution.py:43
  20.9 6.7 %all-to-all-start = ((bf16[16,528,512]{2,1,0:T(8,128)(2,1)}), bf16[16,528,512]{2,1,0:T(8,128)(2,1)}, u32[]{:S(2)}, u32[]{:S(2)}) async-start(bf16[16,528,512]{2,1,0:T(8,128)(2,1)} %bitcast.29), calls=%async_computation | async-start | bytes 17301504 | tf_op jit(solution)/shard_map/all_to_all | solution.py:45
  27.6 151.7 %all-to-all-done = bf16[16,528,512]{2,1,0:T(8,128)(2,1)} async-done(((bf16[16,528,512]{2,1,0:T(8,128)(2,1)}), bf16[16,528,512]{2,1,0:T(8,128)(2,1)}, u32[]{:S(2)}, u32[]{:S(2)}) %all-to-all-start) | async-done | bytes 8650784 | tf_op jit(solution)/shard_map/all_to_all | solution.py:45
  179.3 1.5 fusion.17
  180.8 0.1 reshape.147
  180.9 0.1 fusion.18
  181.0 4.7 %fusion.2 = f32[33,512,8,8,1]{1,3,4,2,0:T(8,128)S(1)} fusion(bf16[32,33,8,512,1]{3,2,1,0,4:T(8,128)(2,1)} %bitcast.7, bf16[32,8]{1,0:T(8,128)(2,1)S(1)} %fusion.18, bf16[8,8]{1,0:T(8,128)(2,1)S(1)} %fusion.20), kind=kOutput, calls=%fused_computation.5 | convolution fusion | flops 553713664 | bytes 12976768 | tf_op jit(solution)/shard_map/irjk,jbkq->birq/dot_general | solution.py:57
  185.6 0.5 slice.46
  186.1 1.1 copy-done.1
  187.2 7.0 %collective-permute-start = (bf16[1,8,512]{2,1,0:T(8,128)(2,1)S(1)}, bf16[1,8,512]{2,1,0:T(8,128)(2,1)S(1)}, u32[]{:S(2)}, u32[]{:S(2)}) collective-permute-start(bf16[1,8,512]{2,1,0:T(8,128)(2,1)S(1)} %get-tuple-element.7), channel_id=1, source_target_pairs={{0,16},{16,32},{32,48},{48,64},{64,80},{80,96},{96,112},{112,128},... | collective-permute-start | bytes 24584 | tf_op jit(solution)/shard_map/ppermute | solution.py:66
  194.3 1.9 collective-permute-start.1
  196.2 0.8 fusion.8
  197.0 3.5 %collective-permute-done.1 = bf16[1,8,512]{2,1,0:T(8,128)(2,1)S(1)} collective-permute-done((bf16[1,8,512]{2,1,0:T(8,128)(2,1)S(1)}, bf16[1,8,512]{2,1,0:T(8,128)(2,1)S(1)}, u32[]{:S(2)}, u32[]{:S(2)}) %collective-permute-start.1) | collective-permute-done | bytes 8224 | tf_op jit(solution)/shard_map/ppermute | solution.py:67
  200.4 0.3 maximum_convert_fusion
  200.8 2.0 fusion.7
  (11 shorter events, 0.1 us)
Async XLA Ops:
  0.0 8.8 %copy-start = (bf16[4,512,512]{2,1,0:T(8,128)(2,1)S(1)}, bf16[4,512,512]{2,1,0:T(8,128)(2,1)}, u32[]{:S(2)}) copy-start(bf16[4,512,512]{2,1,0:T(8,128)(2,1)} %param.7) | copy-start | bytes 6291460
  20.9 158.4 %all-to-all-start = ((bf16[16,528,512]{2,1,0:T(8,128)(2,1)}), bf16[16,528,512]{2,1,0:T(8,128)(2,1)}, u32[]{:S(2)}, u32[]{:S(2)}) async-start(bf16[16,528,512]{2,1,0:T(8,128)(2,1)} %bitcast.29), calls=%async_computation | async-start | bytes 17301504 | tf_op jit(solution)/shard_map/all_to_all | solution.py:45
  185.6 1.6 copy-start.1
  187.2 9.8 %collective-permute-start = (bf16[1,8,512]{2,1,0:T(8,128)(2,1)S(1)}, bf16[1,8,512]{2,1,0:T(8,128)(2,1)S(1)}, u32[]{:S(2)}, u32[]{:S(2)}) collective-permute-start(bf16[1,8,512]{2,1,0:T(8,128)(2,1)S(1)} %get-tuple-element.7), channel_id=1, source_target_pairs={{0,16},{16,32},{32,48},{48,64},{64,80},{80,96},{96,112},{112,128},... | collective-permute-start | bytes 24584 | tf_op jit(solution)/shard_map/ppermute | solution.py:66
  194.3 6.2 %collective-permute-start.1 = (bf16[1,8,512]{2,1,0:T(8,128)(2,1)S(1)}, bf16[1,8,512]{2,1,0:T(8,128)(2,1)S(1)}, u32[]{:S(2)}, u32[]{:S(2)}) collective-permute-start(bf16[1,8,512]{2,1,0:T(8,128)(2,1)S(1)} %get-tuple-element.8), channel_id=1, source_target_pairs={{16,0},{32,16},{48,32},{64,48},{80,64},{96,80},{112,96},{128,112},... | collective-permute-start | bytes 24584 | tf_op jit(solution)/shard_map/ppermute | solution.py:67

commit v6 on v5

--- a/solution.py
+++ b/solution.py
@@ -42,6 +42,9 @@
     pick = jnp.where(jnp.any(chosen, axis=0), jnp.argmax(chosen, axis=0), pair_total)
     outgoing = jnp.take(tagged, pick.reshape(twin_count * slot_count), axis=0, mode="clip")
     outgoing = outgoing.reshape(twin_count, slot_count * (channels + meta_rows), samples)
+    sub = 8
+    same = lax.broadcasted_iota(jnp.int32, (sub, 1, 1, sub), 0) == lax.broadcasted_iota(jnp.int32, (sub, 1, 1, sub), 3)
+    outgoing, same = lax.optimization_barrier((outgoing, same))
     arrived = lax.all_to_all(outgoing, "twin", split_axis=0, concat_axis=0, tiled=True)
     arrived = arrived.reshape(twin_count, slot_count, channels + meta_rows, samples)
 
@@ -50,9 +53,7 @@
 
     sub = 8
     blocks = (channels + meta_rows) // sub
-    spread = jnp.einsum(
-        "jr,ik->irjk", hit.reshape(twin_count * slot_count, rounds), jnp.eye(sub, dtype=jnp.bfloat16)
-    )
+    spread = jnp.where(same, hit.reshape(twin_count * slot_count, rounds).T[None, :, :, None], jnp.zeros((), jnp.bfloat16))
     stacked = arrived.reshape(twin_count * slot_count, blocks, sub, samples)
     noise = jnp.einsum("irjk,jbkq->birq", spread, stacked, preferred_element_type=jnp.float32)
     noise = noise.reshape(blocks * sub, rounds, samples)

time: 204 us -> 151 us (0.74)
  waiting for transfers between devices: 155 us -> 3 us
  blocking collectives: 0 us -> 105 us
  starting transfers between devices: 15.7 us -> 8.96 us
  local copies, waits for them, and re-layouts: 14.5 us -> 16.7 us
    all_to_all x1 -> x0, waiting for transfers between devices: 152 us -> none  [local(): lax.all_to_all(outgoing, 'twin', split_axis=0, concat_axis=0, tiled=True)]
    all_to_all x0 -> x1, blocking collectives: none -> 105 us  [local(): lax.all_to_all(outgoing, 'twin', split_axis=0, concat_axis=0, tiled=True)]
    all_to_all x1 -> x0, starting transfers between devices: 6.75 us -> none  [local(): lax.all_to_all(outgoing, 'twin', split_axis=0, concat_axis=0, tiled=True)]
    unnamed x4 -> x6, local copies, waits for them, and re-layouts: 1.13 us -> 3.3 us
  transfers between devices with their start and end apart: 3 -> 2, of which waited for: 2 -> 1; matrix products, arithmetic and copies ran while one was open for 0% -> 1% of each run, Pallas kernels for 0% -> 0%
where the time goes in v6:
time: 151 us; the launch traced here: 150 us
  blocking collectives  105 us (70%)
  local copies, waits for them, and re-layouts  16.7 us (11%)
  other arithmetic  9.45 us (6%)
  starting transfers between devices  8.96 us (6%)
  matrix products  7.12 us (5%)
  waiting for transfers between devices  3 us (2%)
    all_to_all x1, blocking collectives, local(): lax.all_to_all(outgoing, 'twin', split_axis=0, concat_axis=0, tiled=True)  105 us
    gather x1, local copies, waits for them, and re-layouts, local(): jnp.take(tagged, pick.reshape(twin_count * slot_count), axis=0, mode='clip')  7.28 us
    ppermute x1, starting transfers between devices, local(): low = lax.ppermute(cleaned_rows(channels - 1, channels), 'rcv', forward)  7.04 us
    gather x1, local copies, waits for them, and re-layouts, local(): guides = jnp.take(record, slip_block // twin_count, axis=1, mode='clip')  4.98 us
    dot_general x1, matrix products, local(): jnp.einsum('irjk,jbkq->birq', spread, stacked, preferred_element_type=jnp...  4.78 us
    unnamed x6, local copies, waits for them, and re-layouts  3.3 us
  transfers between devices with their start and end apart: 2, of which 1 were waited for; matrix products, arithmetic and copies ran while one was open for 1% of the time, Pallas kernels for 0%

profile of v6, /device:TPU:97, one launch (start us, length us, event | category | flops | bytes accessed | tf_op | source)
XLA Modules:
  0.0 150.3 jit_solution(14729022239318590221)
XLA Ops:
  0.0 0.8 and_select_fusion.2
  0.8 0.8 subtract_compare_fusion
  1.6 0.8 fusion.22
  2.3 0.1 ge.19
  2.4 0.1 ne.70
  2.5 0.1 rem.46
  2.6 0.1 div.28
  2.7 0.2 convert_reduce_fusion
  2.9 0.1 iota_compare_fusion.3
  3.0 0.1 and_reduce_fusion.1
  3.1 0.6 and_reduce_fusion
  3.7 0.1 copy.9
  3.8 0.1 reshape.171
  3.9 5.0 %gather_fusion = bf16[4,256,512]{2,0,1:T(4,128)(2,1)S(1)} fusion(bf16[256,8,512]{2,1,0:T(8,128)(2,1)} %param.4, s32[1024]{0:T(1024)S(1)} %pad_clamp_fusion.1), kind=kCustom, calls=%fused_computation | custom fusion | bytes 2097168 | tf_op jit(solution)/shard_map/jit(_take)/gather | solution.py:28
  8.9 2.3 %convolution_convert_fusion = bf16[256,4,4,512]{3,0,2,1:T(8,128)(2,1)S(1)} fusion(bf16[4,512,512]{2,1,0:T(8,128)(2,1)S(1)} %copy-done, bf16[256,4,512,1]{2,1,0,3:T(4,128)(2,1)S(1)} %bitcast.34), kind=kOutput, calls=%fused_computation.15 | convolution fusion | flops 2149580800 | bytes 7340032 | tf_op jit(solution)/shard_map/crp,hpq->rhcq/dot_general | solution.py:29
  11.2 0.1 broadcast_in_dim.56
  11.3 2.3 %fusion.4 = bf16[17,264,512]{2,1,0:T(8,128)(2,1)} fusion(bf16[16,8,512]{2,1,0:T(8,128)(2,1)S(1)} %broadcast_in_dim.56, bf16[16,256,512]{2,1,0:T(8,128)(2,1)S(1)} %bitcast.31), kind=kLoop, calls=%fused_computation.7 | loop fusion | flops 16084992 | bytes 8921088 | tf_op jit(solution)/shard_map/concatenate | solution.py:38
  13.6 7.3 %gather_fusion.1 = bf16[32,264,512]{2,1,0:T(8,128)(2,1)} fusion(bf16[17,264,512]{2,1,0:T(8,128)(2,1)} %fusion.4, s32[1024]{0:T(1024)S(1)} %pad_clamp_fusion), kind=kCustom, calls=%fused_computation.1 | custom fusion | bytes 17301632 | tf_op jit(solution)/shard_map/jit(_take)/gather | solution.py:43
  20.9 105.0 %all_to_all.5 = bf16[16,528,512]{2,1,0:T(8,128)(2,1)S(1)} all-to-all(bf16[16,528,512]{2,1,0:T(8,128)(2,1)} %bitcast.28), channel_id=1, replica_groups=mesh['rcv'=16,'twin'=16] {'twin'}, dimensions={0} | all-to-all | bytes 17301504 | tf_op jit(solution)/shard_map/all_to_all | solution.py:48
  125.8 3.3 %copy-done.2 = bf16[16,528,512]{2,1,0:T(8,128)(2,1)} copy-done((bf16[16,528,512]{2,1,0:T(8,128)(2,1)}, bf16[16,528,512]{2,1,0:T(8,128)(2,1)S(1)}, u32[]{:S(2)}) %copy-start.2) | copy-done | bytes 8650776
  129.1 0.6 fusion.18
  129.8 0.1 reshape.160
  129.9 0.1 fusion.19
  129.9 4.8 %fusion.2 = f32[33,512,8,8,1]{1,3,4,2,0:T(8,128)S(1)} fusion(bf16[32,33,8,512,1]{3,2,1,0,4:T(8,128)(2,1)} %bitcast.30, pred[8,8]{1,0:T(8,128)(4,1)S(1)} %bitcast.35, bf16[8,32]{0,1:T(8,128)(2,1)S(1)} %fusion.19), kind=kOutput, calls=%fused_computation.5 | convolution fusion | flops 553664512 | bytes 12976704 | tf_op jit(solution)/shard_map/irjk,jbkq->birq/dot_general | solution.py:58
  134.7 0.0 copy-done.1
  134.8 7.0 %collective-permute-start = (bf16[1,8,512]{2,1,0:T(8,128)(2,1)S(1)}, bf16[1,8,512]{2,1,0:T(8,128)(2,1)S(1)}, u32[]{:S(2)}, u32[]{:S(2)}) collective-permute-start(bf16[1,8,512]{2,1,0:T(8,128)(2,1)S(1)} %get-tuple-element.11), channel_id=1, source_target_pairs={{0,16},{16,32},{32,48},{48,64},{64,80},{80,96},{96,112},{112,128},... | collective-permute-start | bytes 24584 | tf_op jit(solution)/shard_map/ppermute | solution.py:67
  141.8 1.9 %collective-permute-start.1 = (bf16[1,8,512]{2,1,0:T(8,128)(2,1)S(1)}, bf16[1,8,512]{2,1,0:T(8,128)(2,1)S(1)}, u32[]{:S(2)}, u32[]{:S(2)}) collective-permute-start(bf16[1,8,512]{2,1,0:T(8,128)(2,1)S(1)} %get-tuple-element.12), channel_id=1, source_target_pairs={{16,0},{32,16},{48,32},{64,48},{80,64},{96,80},{112,96},{128,112},... | collective-permute-start | bytes 24584 | tf_op jit(solution)/shard_map/ppermute | solution.py:68
  143.7 0.5 slice.46
  144.2 0.8 fusion.8
  145.0 3.0 %collective-permute-done.1 = bf16[1,8,512]{2,1,0:T(8,128)(2,1)S(1)} collective-permute-done((bf16[1,8,512]{2,1,0:T(8,128)(2,1)S(1)}, bf16[1,8,512]{2,1,0:T(8,128)(2,1)S(1)}, u32[]{:S(2)}, u32[]{:S(2)}) %collective-permute-start.1) | collective-permute-done | bytes 8224 | tf_op jit(solution)/shard_map/ppermute | solution.py:68
  148.0 0.3 maximum_convert_fusion
  148.3 2.0 %fusion.7 = bf16[256,8,512]{2,1,0:T(8,128)(2,1)} fusion(f32[258,8,512]{2,1,0:T(8,128)S(1)} %maximum_convert_fusion), kind=kLoop, calls=%fused_computation.11 | loop fusion | flops 5242880 | bytes 14680064 | tf_op jit(solution)/shard_map/convert_element_type | solution.py:72
  (12 shorter events, 0.1 us)
Async XLA Ops:
  0.0 8.8 %copy-start = (bf16[4,512,512]{2,1,0:T(8,128)(2,1)S(1)}, bf16[4,512,512]{2,1,0:T(8,128)(2,1)}, u32[]{:S(2)}) copy-start(bf16[4,512,512]{2,1,0:T(8,128)(2,1)} %param.7) | copy-start | bytes 6291460
  125.8 3.3 %copy-start.2 = (bf16[16,528,512]{2,1,0:T(8,128)(2,1)}, bf16[16,528,512]{2,1,0:T(8,128)(2,1)S(1)}, u32[]{:S(2)}) copy-start(bf16[16,528,512]{2,1,0:T(8,128)(2,1)S(1)} %all_to_all.5) | copy-start | bytes 25952260
  129.9 4.8 %copy-start.1 = (bf16[256,8,512]{2,1,0:T(8,128)(2,1)S(1)}, bf16[256,8,512]{2,1,0:T(8,128)(2,1)}, u32[]{:S(2)}) copy-start(bf16[256,8,512]{2,1,0:T(8,128)(2,1)} %param.4) | copy-start | bytes 6291460
  134.8 10.2 %collective-permute-start = (bf16[1,8,512]{2,1,0:T(8,128)(2,1)S(1)}, bf16[1,8,512]{2,1,0:T(8,128)(2,1)S(1)}, u32[]{:S(2)}, u32[]{:S(2)}) collective-permute-start(bf16[1,8,512]{2,1,0:T(8,128)(2,1)S(1)} %get-tuple-element.11), channel_id=1, source_target_pairs={{0,16},{16,32},{32,48},{48,64},{64,80},{80,96},{96,112},{112,128},... | collective-permute-start | bytes 24584 | tf_op jit(solution)/shard_map/ppermute | solution.py:67
  141.8 6.2 %collective-permute-start.1 = (bf16[1,8,512]{2,1,0:T(8,128)(2,1)S(1)}, bf16[1,8,512]{2,1,0:T(8,128)(2,1)S(1)}, u32[]{:S(2)}, u32[]{:S(2)}) collective-permute-start(bf16[1,8,512]{2,1,0:T(8,128)(2,1)S(1)} %get-tuple-element.12), channel_id=1, source_target_pairs={{16,0},{32,16},{48,32},{64,48},{80,64},{96,80},{112,96},{128,112},... | collective-permute-start | bytes 24584 | tf_op jit(solution)/shard_map/ppermute | solution.py:68

commit v7 on v6

--- a/solution.py
+++ b/solution.py
@@ -61,11 +61,17 @@
     def cleaned_rows(lo, hi):
         return (record[lo:hi].astype(jnp.float32) - noise[lo:hi]).astype(jnp.bfloat16)
 
+    def edge_row(c):
+        edge_noise = jnp.einsum(
+            "nsr,nsq->rq", hit, arrived[:, :, c], preferred_element_type=jnp.float32
+        )
+        return (record[c].astype(jnp.float32) - edge_noise).astype(jnp.bfloat16)[None]
+
     count = lax.axis_size("rcv")
     forward = [(i, i + 1) for i in range(count - 1)]
     backward = [(target, source) for source, target in forward]
-    low = lax.ppermute(cleaned_rows(channels - 1, channels), "rcv", forward)
-    high = lax.ppermute(cleaned_rows(0, 1), "rcv", backward)
+    low = lax.ppermute(edge_row(channels - 1), "rcv", forward)
+    high = lax.ppermute(edge_row(0), "rcv", backward)
     cleaned = cleaned_rows(0, channels)
     widened = jnp.concatenate([low, cleaned, high], axis=0).astype(jnp.float32)
     smooth = 0.5 * widened[1:-1] + 0.25 * (widened[:-2] + widened[2:])

time: 151 us -> 150 us (level)
  waiting for transfers between devices: 3 us -> 0.01 us
  matrix products: 7.12 us -> 8.78 us
    ppermute x2, waiting for transfers between devices: 3 us -> 0.01 us  [the longest x1 0.01 us: local(): high = lax.ppermute(edge_row(0), 'rcv', backward)]
    dot_general x0 -> x2, matrix products: none -> 1.78 us  [edge_row(): jnp.einsum('nsr,nsq->rq', hit, arrived[:, :, c], preferred_element_type=j...]
  transfers between devices with their start and end apart: 2 -> 2, of which waited for: 1 -> 0; matrix products, arithmetic and copies ran while one was open for 1% -> 4% of each run, Pallas kernels for 0% -> 0%
where the time goes in v7:
time: 150 us
  blocking collectives  105 us (70%)
  local copies, waits for them, and re-layouts  17.1 us (11%)
  other arithmetic  9.46 us (6%)
  starting transfers between devices  8.96 us (6%)
  matrix products  8.78 us (6%)
    all_to_all x1, blocking collectives, local(): lax.all_to_all(outgoing, 'twin', split_axis=0, concat_axis=0, tiled=True)  105 us
    gather x1, local copies, waits for them, and re-layouts, local(): jnp.take(tagged, pick.reshape(twin_count * slot_count), axis=0, mode='clip')  7.28 us
    gather x1, local copies, waits for them, and re-layouts, local(): guides = jnp.take(record, slip_block // twin_count, axis=1, mode='clip')  4.78 us
    ppermute x1, starting transfers between devices, local(): low = lax.ppermute(edge_row(channels - 1), 'rcv', forward)  4.65 us
    dot_general x1, matrix products, local(): jnp.einsum('irjk,jbkq->birq', spread, stacked, preferred_element_type=jnp...  4.65 us
    ppermute x1, starting transfers between devices, local(): high = lax.ppermute(edge_row(0), 'rcv', backward)  4.31 us
    unnamed x6, local copies, waits for them, and re-layouts  3.75 us
  transfers between devices with their start and end apart: 2, of which 0 were waited for; matrix products, arithmetic and copies ran while one was open for 4% of the time, Pallas kernels for 0%

profile of v7, /device:TPU:97, one launch (start us, length us, event | category | flops | bytes accessed | tf_op | source)
XLA Modules:
  0.0 149.5 jit_solution(3506703385193674921)
XLA Ops:
  0.0 0.8 and_select_fusion.2
  0.8 0.8 subtract_compare_fusion
  1.6 0.8 fusion.30
  2.3 0.1 ge.19
  2.4 0.1 ne.70
  2.5 0.1 rem.46
  2.6 0.1 div.28
  2.7 0.2 convert_reduce_fusion
  3.0 0.1 and_reduce_fusion.1
  3.1 0.6 and_reduce_fusion
  3.7 0.1 copy.13
  3.8 0.1 reshape.178
  3.9 4.8 %gather_fusion = bf16[4,256,512]{2,0,1:T(4,128)(2,1)S(1)} fusion(bf16[256,8,512]{2,1,0:T(8,128)(2,1)} %param.4, s32[1024]{0:T(1024)S(1)} %pad_clamp_fusion.1), kind=kCustom, calls=%fused_computation | custom fusion | bytes 2097168 | tf_op jit(solution)/shard_map/jit(_take)/gather | solution.py:28
  8.7 2.3 %convolution_convert_fusion = bf16[256,4,4,512]{3,0,2,1:T(8,128)(2,1)S(1)} fusion(bf16[4,512,512]{2,1,0:T(8,128)(2,1)S(1)} %copy-done, bf16[256,4,512,1]{2,1,0,3:T(4,128)(2,1)S(1)} %bitcast.66), kind=kOutput, calls=%fused_computation.15 | convolution fusion | flops 2149580800 | bytes 7340032 | tf_op jit(solution)/shard_map/crp,hpq->rhcq/dot_general | solution.py:29
  11.1 2.3 %fusion.4 = bf16[17,264,512]{2,1,0:T(8,128)(2,1)} fusion(bf16[16,8,512]{2,1,0:T(8,128)(2,1)S(1)} %broadcast_in_dim.62, bf16[16,256,512]{2,1,0:T(8,128)(2,1)S(1)} %bitcast.65), kind=kLoop, calls=%fused_computation.7 | loop fusion | flops 16084992 | bytes 8921088 | tf_op jit(solution)/shard_map/concatenate | solution.py:38
  13.4 7.3 %gather_fusion.1 = bf16[32,264,512]{2,1,0:T(8,128)(2,1)} fusion(bf16[17,264,512]{2,1,0:T(8,128)(2,1)} %fusion.4, s32[1024]{0:T(1024)S(1)} %pad_clamp_fusion), kind=kCustom, calls=%fused_computation.1 | custom fusion | bytes 17301632 | tf_op jit(solution)/shard_map/jit(_take)/gather | solution.py:43
  20.7 105.1 %all_to_all.5 = bf16[16,528,512]{2,1,0:T(8,128)(2,1)S(1)} all-to-all(bf16[16,528,512]{2,1,0:T(8,128)(2,1)} %bitcast.60), channel_id=1, replica_groups=mesh['rcv'=16,'twin'=16] {'twin'}, dimensions={0} | all-to-all | bytes 17301504 | tf_op jit(solution)/shard_map/all_to_all | solution.py:48
  125.7 0.6 fusion.34
  126.4 2.6 %copy-done.2 = bf16[16,528,512]{2,1,0:T(8,128)(2,1)} copy-done((bf16[16,528,512]{2,1,0:T(8,128)(2,1)}, bf16[16,528,512]{2,1,0:T(8,128)(2,1)S(1)}, u32[]{:S(2)}) %copy-start.2) | copy-done | bytes 8650776
  129.0 0.1 fusion.35
  129.1 0.1 reshape.166
  129.3 0.1 copy.14
  129.4 0.9 fusion.18
  130.3 0.9 fusion.17
  131.2 4.3 %collective-permute-start.1 = (bf16[1,8,512]{2,1,0:T(8,128)(2,1)S(1)}, bf16[1,8,512]{2,1,0:T(8,128)(2,1)S(1)}, u32[]{:S(2)}, u32[]{:S(2)}) collective-permute-start(bf16[1,8,512]{2,1,0:T(8,128)(2,1)S(1)} %fusion.17), channel_id=1, source_target_pairs={{16,0},{32,16},{48,32},{64,48},{80,64},{96,80},{112,96},{128,112},... | collective-permute-start | bytes 24584 | tf_op jit(solution)/shard_map/ppermute | solution.py:74
  135.5 4.7 %collective-permute-start = (bf16[1,8,512]{2,1,0:T(8,128)(2,1)S(1)}, bf16[1,8,512]{2,1,0:T(8,128)(2,1)S(1)}, u32[]{:S(2)}, u32[]{:S(2)}) collective-permute-start(bf16[1,8,512]{2,1,0:T(8,128)(2,1)S(1)} %fusion.18), channel_id=1, source_target_pairs={{0,16},{16,32},{32,48},{48,64},{64,80},{80,96},{96,112},{112,128},... | collective-permute-start | bytes 24584 | tf_op jit(solution)/shard_map/ppermute | solution.py:73
  140.2 4.6 %fusion.9 = f32[33,8,8,512]{3,2,1,0:T(8,128)S(1)} fusion(bf16[32,33,8,512,1]{3,2,1,0,4:T(8,128)(2,1)} %bitcast.64, pred[8,8]{1,0:T(8,128)(4,1)S(1)} %bitcast.69, bf16[8,32]{0,1:T(8,128)(2,1)S(1)} %fusion.25), kind=kOutput, calls=%fused_computation.16 | convolution fusion | flops 553664512 | bytes 12976704 | tf_op jit(solution)/shard_map/irjk,jbkq->birq/dot_general | solution.py:58
  144.8 0.5 slice.46
  145.3 1.1 copy-done.1
  146.4 0.8 fusion.8
  147.2 0.3 maximum_convert_fusion
  147.5 2.0 %fusion.7 = bf16[256,8,512]{2,1,0:T(8,128)(2,1)} fusion(f32[258,8,512]{2,1,0:T(8,128)S(1)} %maximum_convert_fusion), kind=kLoop, calls=%fused_computation.11 | loop fusion | flops 5242880 | bytes 14680064 | tf_op jit(solution)/shard_map/convert_element_type | solution.py:78
  (16 shorter events, 0.3 us)
Async XLA Ops:
  0.0 8.6 %copy-start = (bf16[4,512,512]{2,1,0:T(8,128)(2,1)S(1)}, bf16[4,512,512]{2,1,0:T(8,128)(2,1)}, u32[]{:S(2)}) copy-start(bf16[4,512,512]{2,1,0:T(8,128)(2,1)} %param.7) | copy-start | bytes 6291460
  125.7 3.3 %copy-start.2 = (bf16[16,528,512]{2,1,0:T(8,128)(2,1)}, bf16[16,528,512]{2,1,0:T(8,128)(2,1)S(1)}, u32[]{:S(2)}) copy-start(bf16[16,528,512]{2,1,0:T(8,128)(2,1)S(1)} %all_to_all.5) | copy-start | bytes 25952260
  131.2 16.0 %collective-permute-start.1 = (bf16[1,8,512]{2,1,0:T(8,128)(2,1)S(1)}, bf16[1,8,512]{2,1,0:T(8,128)(2,1)S(1)}, u32[]{:S(2)}, u32[]{:S(2)}) collective-permute-start(bf16[1,8,512]{2,1,0:T(8,128)(2,1)S(1)} %fusion.17), channel_id=1, source_target_pairs={{16,0},{32,16},{48,32},{64,48},{80,64},{96,80},{112,96},{128,112},... | collective-permute-start | bytes 24584 | tf_op jit(solution)/shard_map/ppermute | solution.py:74
  135.5 11.7 %collective-permute-start = (bf16[1,8,512]{2,1,0:T(8,128)(2,1)S(1)}, bf16[1,8,512]{2,1,0:T(8,128)(2,1)S(1)}, u32[]{:S(2)}, u32[]{:S(2)}) collective-permute-start(bf16[1,8,512]{2,1,0:T(8,128)(2,1)S(1)} %fusion.18), channel_id=1, source_target_pairs={{0,16},{16,32},{32,48},{48,64},{64,80},{80,96},{96,112},{112,128},... | collective-permute-start | bytes 24584 | tf_op jit(solution)/shard_map/ppermute | solution.py:73
  144.8 1.6 %copy-start.1 = (bf16[256,8,512]{2,1,0:T(8,128)(2,1)S(1)}, bf16[256,8,512]{2,1,0:T(8,128)(2,1)}, u32[]{:S(2)}) copy-start(bf16[256,8,512]{2,1,0:T(8,128)(2,1)} %param.4) | copy-start | bytes 6291460

commit v8 on v7

--- a/solution.py
+++ b/solution.py
@@ -25,7 +25,11 @@
     pair_total = rec_count * order_count
     slot_count = pair_total // twin_count + 1
 
-    guides = jnp.take(record, slip_block // twin_count, axis=1, mode="clip")
+    slip_round = slip_block // twin_count
+    on_round = slip_round[:, None] == jnp.arange(rounds, dtype=jnp.int32)[None, :]
+    guides = jnp.sum(
+        jnp.where(on_round[None, :, :, None], record[:, None, :, :], jnp.zeros((), record.dtype)), axis=2
+    )
     estimates = jnp.einsum(
         "crp,hpq->rhcq", guides, order_ops, preferred_element_type=jnp.float32
     ).astype(jnp.bfloat16)

time: 150 us -> 151 us (level)
  other arithmetic: 9.46 us -> 15.2 us
  local copies, waits for them, and re-layouts: 17.1 us -> 12.4 us
    reduce_sum x0 -> x1, other arithmetic: none -> 5.69 us  [local(): jnp.sum(jnp.where(on_round[None, :, :, None], record[:, None, :, :], jnp....]
    gather x1 -> x0, local copies, waits for them, and re-layouts: 4.78 us -> none  [local(): guides = jnp.take(record, slip_block // twin_count, axis=1, mode='clip')]
where the time goes in v8:
time: 151 us; the launch traced here: 150 us
  blocking collectives  105 us (70%)
  other arithmetic  15.2 us (10%)
  local copies, waits for them, and re-layouts  12.4 us (8%)
  starting transfers between devices  8.99 us (6%)
  matrix products  8.77 us (6%)
    all_to_all x1, blocking collectives, local(): lax.all_to_all(outgoing, 'twin', split_axis=0, concat_axis=0, tiled=True)  105 us
    gather x1, local copies, waits for them, and re-layouts, local(): jnp.take(tagged, pick.reshape(twin_count * slot_count), axis=0, mode='clip')  7.3 us
    reduce_sum x1, other arithmetic, local(): jnp.sum(jnp.where(on_round[None, :, :, None], record[:, None, :, :], jnp....  5.69 us
    ppermute x1, starting transfers between devices, local(): low = lax.ppermute(edge_row(channels - 1), 'rcv', forward)  4.66 us
    dot_general x1, matrix products, local(): jnp.einsum('irjk,jbkq->birq', spread, stacked, preferred_element_type=jnp...  4.65 us
    ppermute x1, starting transfers between devices, local(): high = lax.ppermute(edge_row(0), 'rcv', backward)  4.32 us
    unnamed x6, local copies, waits for them, and re-layouts  3.75 us
  transfers between devices with their start and end apart: 2, of which 0 were waited for; matrix products, arithmetic and copies ran while one was open for 4% of the time, Pallas kernels for 0%

profile of v8, /device:TPU:97, one launch (start us, length us, event | category | flops | bytes accessed | tf_op | source)
XLA Modules:
  0.0 150.3 jit_solution(16016715302846141632)
XLA Ops:
  0.0 0.8 and_select_fusion.2
  0.8 0.8 subtract_compare_fusion
  1.6 0.8 fusion.30
  2.3 0.1 ge.19
  2.4 0.1 ne.70
  2.5 0.1 rem.46
  2.6 0.1 div.28
  2.7 0.2 convert_reduce_fusion
  3.0 0.1 and_reduce_fusion.1
  3.1 0.6 and_reduce_fusion
  3.7 0.1 copy.11
  3.8 0.1 reshape.192
  3.9 5.7 %select_reduce_fusion = bf16[256,4,512]{2,1,0:T(4,128)(2,1)S(1)} fusion(pred[4,8]{1,0:T(4,128)(4,1)S(1)} %iota_compare_fusion.8, bf16[256,8,512]{2,1,0:T(8,128)(2,1)} %param.4), kind=kLoop, calls=%fused_computation.6 | loop fusion | flops 7864320 | bytes 3145760 | tf_op jit(solution)/shard_map/reduce_sum | solution.py:30
  9.6 2.3 %convolution_convert_fusion = bf16[256,4,4,512]{3,0,2,1:T(8,128)(2,1)S(1)} fusion(bf16[4,512,512]{2,1,0:T(8,128)(2,1)S(1)} %copy-done, bf16[256,4,512,1]{2,1,0,3:T(4,128)(2,1)S(1)} %bitcast.64), kind=kOutput, calls=%fused_computation.15 | convolution fusion | flops 2149580800 | bytes 7340032 | tf_op jit(solution)/shard_map/crp,hpq->rhcq/dot_general | solution.py:33
  12.1 2.3 %fusion.4 = bf16[17,264,512]{2,1,0:T(8,128)(2,1)} fusion(bf16[16,8,512]{2,1,0:T(8,128)(2,1)S(1)} %broadcast_in_dim.84, bf16[16,256,512]{2,1,0:T(8,128)(2,1)S(1)} %bitcast.63), kind=kLoop, calls=%fused_computation.7 | loop fusion | flops 16084992 | bytes 8921088 | tf_op jit(solution)/shard_map/concatenate | solution.py:42
  14.4 7.3 %gather_fusion = bf16[32,264,512]{2,1,0:T(8,128)(2,1)} fusion(bf16[17,264,512]{2,1,0:T(8,128)(2,1)} %fusion.4, s32[1024]{0:T(1024)S(1)} %pad_clamp_fusion), kind=kCustom, calls=%fused_computation | custom fusion | bytes 17301632 | tf_op jit(solution)/shard_map/jit(_take)/gather | solution.py:47
  21.7 104.8 %all_to_all.5 = bf16[16,528,512]{2,1,0:T(8,128)(2,1)S(1)} all-to-all(bf16[16,528,512]{2,1,0:T(8,128)(2,1)} %bitcast.58), channel_id=1, replica_groups=mesh['rcv'=16,'twin'=16] {'twin'}, dimensions={0} | all-to-all | bytes 17301504 | tf_op jit(solution)/shard_map/all_to_all | solution.py:52
  126.4 0.6 fusion.34
  127.1 2.6 %copy-done.1 = bf16[16,528,512]{2,1,0:T(8,128)(2,1)} copy-done((bf16[16,528,512]{2,1,0:T(8,128)(2,1)}, bf16[16,528,512]{2,1,0:T(8,128)(2,1)S(1)}, u32[]{:S(2)}) %copy-start.1) | copy-done | bytes 8650776
  129.7 0.1 fusion.35
  129.8 0.1 reshape.188
  130.0 0.1 copy.12
  130.1 0.9 fusion.18
  131.0 0.9 fusion.17
  131.9 4.3 %collective-permute-start.1 = (bf16[1,8,512]{2,1,0:T(8,128)(2,1)S(1)}, bf16[1,8,512]{2,1,0:T(8,128)(2,1)S(1)}, u32[]{:S(2)}, u32[]{:S(2)}) collective-permute-start(bf16[1,8,512]{2,1,0:T(8,128)(2,1)S(1)} %fusion.17), channel_id=1, source_target_pairs={{16,0},{32,16},{48,32},{64,48},{80,64},{96,80},{112,96},{128,112},... | collective-permute-start | bytes 24584 | tf_op jit(solution)/shard_map/ppermute | solution.py:78
  136.2 4.7 %collective-permute-start = (bf16[1,8,512]{2,1,0:T(8,128)(2,1)S(1)}, bf16[1,8,512]{2,1,0:T(8,128)(2,1)S(1)}, u32[]{:S(2)}, u32[]{:S(2)}) collective-permute-start(bf16[1,8,512]{2,1,0:T(8,128)(2,1)S(1)} %fusion.18), channel_id=1, source_target_pairs={{0,16},{16,32},{32,48},{48,64},{64,80},{80,96},{96,112},{112,128},... | collective-permute-start | bytes 24584 | tf_op jit(solution)/shard_map/ppermute | solution.py:77
  140.9 4.7 %fusion.9 = f32[33,8,8,512]{3,2,1,0:T(8,128)S(1)} fusion(bf16[32,33,8,512,1]{3,2,1,0,4:T(8,128)(2,1)} %bitcast.62, pred[8,8]{1,0:T(8,128)(4,1)S(1)} %bitcast.67, bf16[8,32]{0,1:T(8,128)(2,1)S(1)} %fusion.25), kind=kOutput, calls=%fused_computation.16 | convolution fusion | flops 553664512 | bytes 12976704 | tf_op jit(solution)/shard_map/irjk,jbkq->birq/dot_general | solution.py:62
  145.5 0.5 slice.44
  146.0 1.1 copy-done.2
  147.1 0.8 fusion.8
  147.9 0.3 maximum_convert_fusion
  148.3 2.0 %fusion.7 = bf16[256,8,512]{2,1,0:T(8,128)(2,1)} fusion(f32[258,8,512]{2,1,0:T(8,128)S(1)} %maximum_convert_fusion), kind=kLoop, calls=%fused_computation.11 | loop fusion | flops 5242880 | bytes 14680064 | tf_op jit(solution)/shard_map/convert_element_type | solution.py:82
  (16 shorter events, 0.4 us)
Async XLA Ops:
  0.0 9.6 %copy-start = (bf16[4,512,512]{2,1,0:T(8,128)(2,1)S(1)}, bf16[4,512,512]{2,1,0:T(8,128)(2,1)}, u32[]{:S(2)}) copy-start(bf16[4,512,512]{2,1,0:T(8,128)(2,1)} %param.7) | copy-start | bytes 6291460
  126.4 3.3 %copy-start.1 = (bf16[16,528,512]{2,1,0:T(8,128)(2,1)}, bf16[16,528,512]{2,1,0:T(8,128)(2,1)S(1)}, u32[]{:S(2)}) copy-start(bf16[16,528,512]{2,1,0:T(8,128)(2,1)S(1)} %all_to_all.5) | copy-start | bytes 25952260
  131.9 16.0 %collective-permute-start.1 = (bf16[1,8,512]{2,1,0:T(8,128)(2,1)S(1)}, bf16[1,8,512]{2,1,0:T(8,128)(2,1)S(1)}, u32[]{:S(2)}, u32[]{:S(2)}) collective-permute-start(bf16[1,8,512]{2,1,0:T(8,128)(2,1)S(1)} %fusion.17), channel_id=1, source_target_pairs={{16,0},{32,16},{48,32},{64,48},{80,64},{96,80},{112,96},{128,112},... | collective-permute-start | bytes 24584 | tf_op jit(solution)/shard_map/ppermute | solution.py:78
  136.2 11.7 %collective-permute-start = (bf16[1,8,512]{2,1,0:T(8,128)(2,1)S(1)}, bf16[1,8,512]{2,1,0:T(8,128)(2,1)S(1)}, u32[]{:S(2)}, u32[]{:S(2)}) collective-permute-start(bf16[1,8,512]{2,1,0:T(8,128)(2,1)S(1)} %fusion.18), channel_id=1, source_target_pairs={{0,16},{16,32},{32,48},{48,64},{64,80},{80,96},{96,112},{112,128},... | collective-permute-start | bytes 24584 | tf_op jit(solution)/shard_map/ppermute | solution.py:77
  145.5 1.6 %copy-start.2 = (bf16[256,8,512]{2,1,0:T(8,128)(2,1)S(1)}, bf16[256,8,512]{2,1,0:T(8,128)(2,1)}, u32[]{:S(2)}) copy-start(bf16[256,8,512]{2,1,0:T(8,128)(2,1)} %param.4) | copy-start | bytes 6291460

commit v9 on v7

--- a/solution.py
+++ b/solution.py
@@ -1,6 +1,8 @@
 import jax
 import jax.numpy as jnp
 from jax import lax
+from jax.experimental import pallas as pl
+from jax.experimental.pallas import tpu as pltpu
 from jax.sharding import PartitionSpec as P
 
 
@@ -16,6 +18,59 @@
     earlier = (owner[None, :] == owner[:, None]) & (position[None, :] < position[:, None])
     slot = jnp.sum(earlier.astype(jnp.int32), axis=1)
     return owner, slot, land_round
+
+
+def place_clean_smooth(spread, arrived, record, channel_block, sub):
+    slots, _, samples = arrived.shape
+    channels, rounds, _ = record.shape
+    steps = channels // channel_block
+
+    def kernel(spread_ref, arrived_ref, record_ref, out_ref, edge_ref, scratch_ref):
+        t = pl.program_id(0)
+        for g in range(channel_block // sub):
+            panel_rows = arrived_ref[:, g * sub : (g + 1) * sub, :].reshape(slots * sub, samples)
+            noise = jnp.dot(spread_ref[...], panel_rows, preferred_element_type=jnp.float32)
+            noise = noise.reshape(sub, rounds, samples)
+            rec = record_ref[g * sub : (g + 1) * sub].astype(jnp.float32)
+            cleaned = (rec - noise).astype(jnp.bfloat16).astype(jnp.float32)
+            scratch_ref[pl.ds(1 + t * channel_block + g * sub, sub)] = cleaned
+
+        @pl.when(t == steps - 1)
+        def _():
+            scratch_ref[0] = jnp.zeros((rounds, samples), jnp.float32)
+            scratch_ref[channels + 1] = jnp.zeros((rounds, samples), jnp.float32)
+
+            def body(i, carry):
+                lo = i * sub
+                mid = scratch_ref[pl.ds(lo + 1, sub)]
+                up = scratch_ref[pl.ds(lo, sub)]
+                down = scratch_ref[pl.ds(lo + 2, sub)]
+                out_ref[pl.ds(lo, sub)] = (0.5 * mid + 0.25 * (up + down)).astype(out_ref.dtype)
+                return carry
+
+            lax.fori_loop(0, channels // sub, body, 0)
+            edge_ref[0:2] = scratch_ref[1:3]
+            edge_ref[2:4] = scratch_ref[channels - 1 : channels + 1]
+
+    return pl.pallas_call(
+        kernel,
+        grid=(steps,),
+        in_specs=[
+            pl.BlockSpec(spread.shape, lambda t: (0, 0)),
+            pl.BlockSpec((slots, channel_block, samples), lambda t: (0, t, 0)),
+            pl.BlockSpec((channel_block, rounds, samples), lambda t: (t, 0, 0)),
+        ],
+        out_specs=[
+            pl.BlockSpec((channels, rounds, samples), lambda t: (0, 0, 0)),
+            pl.BlockSpec((4, rounds, samples), lambda t: (0, 0, 0)),
+        ],
+        out_shape=[
+            jax.ShapeDtypeStruct((channels, rounds, samples), jnp.bfloat16),
+            jax.ShapeDtypeStruct((4, rounds, samples), jnp.float32),
+        ],
+        scratch_shapes=[pltpu.VMEM((channels + 2, rounds, samples), jnp.float32)],
+        compiler_params=pltpu.CompilerParams(dimension_semantics=("arbitrary",)),
+    )(spread, arrived, record)
 
 
 def local(record, slip_block, ghost_lag, order_ops):
@@ -42,7 +97,7 @@
     pick = jnp.where(jnp.any(chosen, axis=0), jnp.argmax(chosen, axis=0), pair_total)
     outgoing = jnp.take(tagged, pick.reshape(twin_count * slot_count), axis=0, mode="clip")
     outgoing = outgoing.reshape(twin_count, slot_count * (channels + meta_rows), samples)
-    sub = 8
+    sub = 16
     same = lax.broadcasted_iota(jnp.int32, (sub, 1, 1, sub), 0) == lax.broadcasted_iota(jnp.int32, (sub, 1, 1, sub), 3)
     outgoing, same = lax.optimization_barrier((outgoing, same))
     arrived = lax.all_to_all(outgoing, "twin", split_axis=0, concat_axis=0, tiled=True)
@@ -51,15 +106,8 @@
     arrived_rounds = arrived[:, :, channels, 0].astype(jnp.int32)
     hit = (arrived_rounds[:, :, None] == jnp.arange(rounds, dtype=jnp.int32)[None, None, :]).astype(jnp.bfloat16)
 
-    sub = 8
-    blocks = (channels + meta_rows) // sub
     spread = jnp.where(same, hit.reshape(twin_count * slot_count, rounds).T[None, :, :, None], jnp.zeros((), jnp.bfloat16))
-    stacked = arrived.reshape(twin_count * slot_count, blocks, sub, samples)
-    noise = jnp.einsum("irjk,jbkq->birq", spread, stacked, preferred_element_type=jnp.float32)
-    noise = noise.reshape(blocks * sub, rounds, samples)
-
-    def cleaned_rows(lo, hi):
-        return (record[lo:hi].astype(jnp.float32) - noise[lo:hi]).astype(jnp.bfloat16)
+    spread = spread.reshape(sub * rounds, twin_count * slot_count * sub)
 
     def edge_row(c):
         edge_noise = jnp.einsum(
@@ -72,10 +120,12 @@
     backward = [(target, source) for source, target in forward]
     low = lax.ppermute(edge_row(channels - 1), "rcv", forward)
     high = lax.ppermute(edge_row(0), "rcv", backward)
-    cleaned = cleaned_rows(0, channels)
-    widened = jnp.concatenate([low, cleaned, high], axis=0).astype(jnp.float32)
-    smooth = 0.5 * widened[1:-1] + 0.25 * (widened[:-2] + widened[2:])
-    return smooth.astype(jnp.bfloat16)
+    slots_view = arrived.reshape(twin_count * slot_count, channels + meta_rows, samples)
+    smooth, edges = place_clean_smooth(spread, slots_view, record, 32, sub)
+    first = 0.5 * edges[0] + 0.25 * (low[0].astype(jnp.float32) + edges[1])
+    last = 0.5 * edges[3] + 0.25 * (edges[2] + high[0].astype(jnp.float32))
+    smooth = smooth.at[0].set(first.astype(jnp.bfloat16)).at[channels - 1].set(last.astype(jnp.bfloat16))
+    return smooth
 
 
 def solution(mesh):

time: 150 us -> 155 us (1.033)
  Pallas kernels: 0 us -> 9.14 us
  matrix products: 8.78 us -> 4.11 us
    pallas_call x0 -> x1, Pallas kernels: none -> 9.14 us  [place_clean_smooth(): pl.pallas_call(kernel, grid=(steps,), in_specs=[pl.BlockSpec(spread.shape...]
    dot_general x1 -> x0, matrix products: 4.65 us -> none  [local(): jnp.einsum('irjk,jbkq->birq', spread, stacked, preferred_element_type=jnp...]
    convert_element_type x3 -> x0, other arithmetic: 3.09 us -> none  [the longest x1 1.99 us: local(): return smooth.astype(jnp.bfloat16)]
    scatter x0 -> x2, other arithmetic: none -> 2.68 us  [local(): smooth.at[0].set(first.astype(jnp.bfloat16)).at[channels - 1]]
    select_n x0 -> x1, local copies, waits for them, and re-layouts: none -> 2.44 us  [local(): jnp.where(same, hit.reshape(twin_count * slot_count, rounds).T[None, :, :...]
    ppermute x1, starting transfers between devices: 4.31 us -> 1.92 us  [local(): high = lax.ppermute(edge_row(0), 'rcv', backward)]
    ppermute x1, starting transfers between devices: 4.65 us -> 7.03 us  [local(): low = lax.ppermute(edge_row(channels - 1), 'rcv', forward)]
    unnamed x6 -> x4, local copies, waits for them, and re-layouts: 3.75 us -> 2.62 us
  transfers between devices with their start and end apart: 2 -> 2, of which waited for: 0 -> 0; matrix products, arithmetic and copies ran while one was open for 4% -> 3% of each run, Pallas kernels for 0% -> 6%
where the time goes in v9:
time: 155 us
  blocking collectives  105 us (68%)
  local copies, waits for them, and re-layouts  18.2 us (12%)
  other arithmetic  9.14 us (6%)
  Pallas kernels  9.14 us (6%)
  starting transfers between devices  8.95 us (6%)
  matrix products  4.11 us (3%)
    all_to_all x1, blocking collectives, local(): lax.all_to_all(outgoing, 'twin', split_axis=0, concat_axis=0, tiled=True)  105 us
    pallas_call x1, Pallas kernels, place_clean_smooth(): pl.pallas_call(kernel, grid=(steps,), in_specs=[pl.BlockSpec(spread.shape...  9.14 us
    gather x1, local copies, waits for them, and re-layouts, local(): jnp.take(tagged, pick.reshape(twin_count * slot_count), axis=0, mode='clip')  7.3 us
    ppermute x1, starting transfers between devices, local(): low = lax.ppermute(edge_row(channels - 1), 'rcv', forward)  7.03 us
    gather x1, local copies, waits for them, and re-layouts, local(): guides = jnp.take(record, slip_block // twin_count, axis=1, mode='clip')  4.97 us
  transfers between devices with their start and end apart: 2, of which 0 were waited for; matrix products, arithmetic and copies ran while one was open for 3% of the time, Pallas kernels for 6%

profile of v9, /device:TPU:97, one launch (start us, length us, event | category | flops | bytes accessed | tf_op | source)
XLA Modules:
  0.0 154.5 jit_solution(17406721971122656766)
XLA Ops:
  0.0 0.8 and_select_fusion.2
  0.8 0.8 subtract_compare_fusion
  1.6 0.8 fusion.18
  2.3 0.1 ge.19
  2.4 0.1 ne.70
  2.5 0.1 rem.46
  2.6 0.1 div.28
  2.7 0.2 convert_reduce_fusion
  3.0 0.1 and_reduce_fusion.1
  3.1 0.6 and_reduce_fusion
  3.7 0.1 copy.12
  3.8 0.1 reshape.239
  3.9 5.0 %gather_fusion = bf16[4,256,512]{2,0,1:T(4,128)(2,1)S(1)} fusion(bf16[256,8,512]{2,1,0:T(8,128)(2,1)} %record_ref.1, s32[1024]{0:T(1024)S(1)} %pad_clamp_fusion.1), kind=kCustom, calls=%fused_computation | custom fusion | bytes 2097168 | tf_op jit(solution)/shard_map/jit(_take)/gather | solution.py:83
  8.8 2.3 %convolution_convert_fusion = bf16[256,4,4,512]{3,0,2,1:T(8,128)(2,1)S(1)} fusion(bf16[4,512,512]{2,1,0:T(8,128)(2,1)S(1)} %copy-done, bf16[256,4,512,1]{2,1,0,3:T(4,128)(2,1)S(1)} %bitcast.54), kind=kOutput, calls=%fused_computation.6 | convolution fusion | flops 2149580800 | bytes 7340032 | tf_op jit(solution)/shard_map/crp,hpq->rhcq/dot_general | solution.py:84
  11.2 0.1 broadcast_in_dim.62
  11.3 2.3 %fusion.2 = bf16[17,264,512]{2,1,0:T(8,128)(2,1)} fusion(bf16[16,8,512]{2,1,0:T(8,128)(2,1)S(1)} %broadcast_in_dim.62, bf16[16,256,512]{2,1,0:T(8,128)(2,1)S(1)} %bitcast.53), kind=kLoop, calls=%fused_computation.5 | loop fusion | flops 16084992 | bytes 8921088 | tf_op jit(solution)/shard_map/concatenate | solution.py:93
  13.6 7.3 %gather_fusion.1 = bf16[32,264,512]{2,1,0:T(8,128)(2,1)} fusion(bf16[17,264,512]{2,1,0:T(8,128)(2,1)} %fusion.2, s32[1024]{0:T(1024)S(1)} %pad_clamp_fusion), kind=kCustom, calls=%fused_computation.1 | custom fusion | bytes 17301632 | tf_op jit(solution)/shard_map/jit(_take)/gather | solution.py:98
  20.9 104.9 %all_to_all.5 = bf16[16,528,512]{2,1,0:T(8,128)(2,1)S(1)} all-to-all(bf16[16,528,512]{2,1,0:T(8,128)(2,1)} %bitcast.52), channel_id=1, replica_groups=mesh['rcv'=16,'twin'=16] {'twin'}, dimensions={0} | all-to-all | bytes 17301504 | tf_op jit(solution)/shard_map/all_to_all | solution.py:103
  125.8 0.6 fusion.21
  126.4 2.6 %copy-done.1 = bf16[16,528,512]{2,1,0:T(8,128)(2,1)} copy-done((bf16[16,528,512]{2,1,0:T(8,128)(2,1)}, bf16[16,528,512]{2,1,0:T(8,128)(2,1)S(1)}, u32[]{:S(2)}) %copy-start.1) | copy-done | bytes 8650776
  129.1 0.1 fusion.22
  129.2 0.1 reshape.225
  129.3 0.1 copy.13
  129.4 0.9 fusion.8
  130.2 0.9 fusion.9
  131.1 7.0 %collective-permute-start = (bf16[1,8,512]{2,1,0:T(8,128)(2,1)S(1)}, bf16[1,8,512]{2,1,0:T(8,128)(2,1)S(1)}, u32[]{:S(2)}, u32[]{:S(2)}) collective-permute-start(bf16[1,8,512]{2,1,0:T(8,128)(2,1)S(1)} %fusion.9), channel_id=1, source_target_pairs={{0,16},{16,32},{32,48},{48,64},{64,80},{80,96},{96,112},{112,128},... | collective-permute-start | bytes 24584 | tf_op jit(solution)/shard_map/ppermute | solution.py:121
  138.2 1.9 %collective-permute-start.1 = (bf16[1,8,512]{2,1,0:T(8,128)(2,1)S(1)}, bf16[1,8,512]{2,1,0:T(8,128)(2,1)S(1)}, u32[]{:S(2)}, u32[]{:S(2)}) collective-permute-start(bf16[1,8,512]{2,1,0:T(8,128)(2,1)S(1)} %fusion.8), channel_id=1, source_target_pairs={{16,0},{32,16},{48,32},{64,48},{80,64},{96,80},{112,96},{128,112},... | collective-permute-start | bytes 24584 | tf_op jit(solution)/shard_map/ppermute | solution.py:122
  140.1 0.2 broadcast_select_fusion
  140.3 2.4 %select_n.71.spread_ref = bf16[128,512]{1,0:T(8,128)(2,1)} reshape(bf16[16,8,32,16]{3,2,1,0:T(8,128)(2,1)S(1)} %broadcast_select_fusion) | data formatting | bytes 262144 | tf_op jit(solution)/shard_map/jit(_where)/select_n | solution.py:109
  142.7 9.1 %shard_map.46 = (bf16[256,8,512]{2,1,0:T(8,128)(2,1)}, f32[4,8,512]{2,1,0:T(8,128)}) custom-call(bf16[128,512]{1,0:T(8,128)(2,1)} %select_n.71.spread_ref, bf16[32,264,512]{2,1,0:T(8,128)(2,1)} %bitcast.51, bf16[256,8,512]{2,1,0:T(8,128)(2,1)} %record_ref.1), custom_call_target="tpu_custom_call" | custom-call | tf_op jit(solution)/shard_map/pallas_call | solution.py:55
  151.8 1.3 fusion.11
  153.2 1.3 fusion.12
  (14 shorter events, 0.2 us)
Async XLA Ops:
  0.0 8.8 %copy-start = (bf16[4,512,512]{2,1,0:T(8,128)(2,1)S(1)}, bf16[4,512,512]{2,1,0:T(8,128)(2,1)}, u32[]{:S(2)}) copy-start(bf16[4,512,512]{2,1,0:T(8,128)(2,1)} %param.11) | copy-start | bytes 6291460
  125.8 3.3 %copy-start.1 = (bf16[16,528,512]{2,1,0:T(8,128)(2,1)}, bf16[16,528,512]{2,1,0:T(8,128)(2,1)S(1)}, u32[]{:S(2)}) copy-start(bf16[16,528,512]{2,1,0:T(8,128)(2,1)S(1)} %all_to_all.5) | copy-start | bytes 25952260
  131.1 20.7 %collective-permute-start = (bf16[1,8,512]{2,1,0:T(8,128)(2,1)S(1)}, bf16[1,8,512]{2,1,0:T(8,128)(2,1)S(1)}, u32[]{:S(2)}, u32[]{:S(2)}) collective-permute-start(bf16[1,8,512]{2,1,0:T(8,128)(2,1)S(1)} %fusion.9), channel_id=1, source_target_pairs={{0,16},{16,32},{32,48},{48,64},{64,80},{80,96},{96,112},{112,128},... | collective-permute-start | bytes 24584 | tf_op jit(solution)/shard_map/ppermute | solution.py:121
  138.2 15.0 %collective-permute-start.1 = (bf16[1,8,512]{2,1,0:T(8,128)(2,1)S(1)}, bf16[1,8,512]{2,1,0:T(8,128)(2,1)S(1)}, u32[]{:S(2)}, u32[]{:S(2)}) collective-permute-start(bf16[1,8,512]{2,1,0:T(8,128)(2,1)S(1)} %fusion.8), channel_id=1, source_target_pairs={{16,0},{32,16},{48,32},{64,48},{80,64},{96,80},{112,96},{128,112},... | collective-permute-start | bytes 24584 | tf_op jit(solution)/shard_map/ppermute | solution.py:122

commit v10 on v7

--- a/solution.py
+++ b/solution.py
@@ -25,31 +25,37 @@
     pair_total = rec_count * order_count
     slot_count = pair_total // twin_count + 1
 
-    guides = jnp.take(record, slip_block // twin_count, axis=1, mode="clip")
-    estimates = jnp.einsum(
-        "crp,hpq->rhcq", guides, order_ops, preferred_element_type=jnp.float32
-    ).astype(jnp.bfloat16)
-    estimates = estimates.reshape(pair_total, channels, samples)
-
     owner, slot, land_round = pair_routes(slip_block, ghost_lag, twin_count)
     meta_rows = 8
-    meta = jnp.broadcast_to(land_round.astype(jnp.bfloat16)[:, None, None], (pair_total, meta_rows, samples))
-    blank = jnp.zeros((1, channels + meta_rows, samples), jnp.bfloat16)
-    tagged = jnp.concatenate([jnp.concatenate([estimates, meta], axis=1), blank], axis=0)
+    guides = jnp.take(record, slip_block // twin_count, axis=1, mode="clip")
+    guides = jnp.pad(guides, ((0, meta_rows), (0, 0), (0, 0)))
+    tags = jnp.stack([land_round, owner, slot], axis=1).astype(jnp.float32)
+    tags = jnp.pad(tags, ((0, 0), (channels, meta_rows - tags.shape[1])))
+    tags = tags.reshape(rec_count, order_count, channels + meta_rows)[:, :, :, None]
+    estimates = (
+        jnp.einsum("crp,hpq->rhcq", guides, order_ops, preferred_element_type=jnp.float32) + tags
+    ).astype(jnp.bfloat16)
+    tagged = estimates.reshape(pair_total, channels + meta_rows, samples)
     chosen = (owner[:, None, None] == jnp.arange(twin_count, dtype=jnp.int32)[None, :, None]) & (
         slot[:, None, None] == jnp.arange(slot_count, dtype=jnp.int32)[None, None, :]
     )
-    pick = jnp.where(jnp.any(chosen, axis=0), jnp.argmax(chosen, axis=0), pair_total)
+    pick = jnp.argmax(chosen, axis=0)
     outgoing = jnp.take(tagged, pick.reshape(twin_count * slot_count), axis=0, mode="clip")
     outgoing = outgoing.reshape(twin_count, slot_count * (channels + meta_rows), samples)
     sub = 8
     same = lax.broadcasted_iota(jnp.int32, (sub, 1, 1, sub), 0) == lax.broadcasted_iota(jnp.int32, (sub, 1, 1, sub), 3)
-    outgoing, same = lax.optimization_barrier((outgoing, same))
+    me = lax.axis_index("twin")
+    outgoing, same, me = lax.optimization_barrier((outgoing, same, me))
     arrived = lax.all_to_all(outgoing, "twin", split_axis=0, concat_axis=0, tiled=True)
     arrived = arrived.reshape(twin_count, slot_count, channels + meta_rows, samples)
 
-    arrived_rounds = arrived[:, :, channels, 0].astype(jnp.int32)
-    hit = (arrived_rounds[:, :, None] == jnp.arange(rounds, dtype=jnp.int32)[None, None, :]).astype(jnp.bfloat16)
+    arrived_tags = arrived[:, :, channels : channels + 3, 0].astype(jnp.int32)
+    kept = (arrived_tags[:, :, 1] == me) & (
+        arrived_tags[:, :, 2] == jnp.arange(slot_count, dtype=jnp.int32)[None, :]
+    )
+    hit = (
+        kept[:, :, None] & (arrived_tags[:, :, 0][:, :, None] == jnp.arange(rounds, dtype=jnp.int32)[None, None, :])
+    ).astype(jnp.bfloat16)
 
     sub = 8
     blocks = (channels + meta_rows) // sub

time: 150 us -> 151 us (level)
  other arithmetic: 9.46 us -> 6.44 us
  local copies, waits for them, and re-layouts: 17.1 us -> 19.7 us
  matrix products: 8.78 us -> 10.4 us
    concatenate x1 -> x0, other arithmetic: 2.3 us -> none  [local(): jnp.concatenate([estimates, meta], axis=1)]
    dot_general x1, matrix products: 2.35 us -> 3.97 us  [local(): jnp.einsum('crp,hpq->rhcq', guides, order_ops, preferred_element_type=jnp...]
    unnamed x6 -> x8, local copies, waits for them, and re-layouts: 3.75 us -> 4.64 us
    gather x1 -> x2, local copies, waits for them, and re-layouts: 4.78 us -> 5.14 us  [local(): guides = jnp.take(record, slip_block // twin_count, axis=1, mode='clip')]
where the time goes in v10:
time: 151 us; the launch traced here: 150 us
  blocking collectives  105 us (70%)
  local copies, waits for them, and re-layouts  19.7 us (13%)
  matrix products  10.4 us (7%)
  starting transfers between devices  8.96 us (6%)
  other arithmetic  6.44 us (4%)
    all_to_all x1, blocking collectives, local(): lax.all_to_all(outgoing, 'twin', split_axis=0, concat_axis=0, tiled=True)  105 us
    gather x1, local copies, waits for them, and re-layouts, local(): jnp.take(tagged, pick.reshape(twin_count * slot_count), axis=0, mode='clip')  7.2 us
    gather x2, local copies, waits for them, and re-layouts, local(): guides = jnp.take(record, slip_block // twin_count, axis=1, mode='clip')  5.14 us
    ppermute x1, starting transfers between devices, local(): low = lax.ppermute(edge_row(channels - 1), 'rcv', forward)  4.65 us
    dot_general x1, matrix products, local(): jnp.einsum('irjk,jbkq->birq', spread, stacked, preferred_element_type=jnp...  4.65 us
    unnamed x8, local copies, waits for them, and re-layouts  4.64 us
    ppermute x1, starting transfers between devices, local(): high = lax.ppermute(edge_row(0), 'rcv', backward)  4.31 us
    dot_general x1, matrix products, local(): jnp.einsum('crp,hpq->rhcq', guides, order_ops, preferred_element_type=jnp...  3.97 us
  transfers between devices with their start and end apart: 2, of which 0 were waited for; matrix products, arithmetic and copies ran while one was open for 4% of the time, Pallas kernels for 0%

profile of v10, /device:TPU:97, one launch (start us, length us, event | category | flops | bytes accessed | tf_op | source)
XLA Modules:
  0.0 150.5 jit_solution(5016122880008239977)
XLA Ops:
  0.0 0.8 and_select_fusion.3
  0.8 0.8 sign_compare_fusion
  1.6 0.1 ge.27
  1.7 0.1 ge.26
  1.8 0.8 fusion.34
  2.5 0.1 rem.52
  2.7 0.2 convert_reduce_fusion
  2.9 0.1 ne.84
  3.2 0.1 copy.42
  3.2 0.6 iota_reduce_fusion
  3.9 0.1 reshape.219
  4.1 4.9 %gather_fusion = bf16[4,256,512]{2,0,1:T(4,128)(2,1)S(1)} fusion(bf16[256,8,512]{2,1,0:T(8,128)(2,1)} %param.4, s32[1024]{0:T(1024)S(1)} %pad_clamp_fusion.1), kind=kCustom, calls=%fused_computation | custom fusion | bytes 2097168 | tf_op jit(solution)/shard_map/jit(_take)/gather | solution.py:30
  9.0 0.2 copy.52
  9.2 4.0 %fusion.2 = bf16[4,4,264,512]{3,2,1,0:T(8,128)(2,1)} fusion(f32[4,4,264]{2,1,0:T(4,128)S(1)} %add.55, bf16[4,512,512]{2,1,0:T(8,128)(2,1)S(1)} %copy-done, bf16[256,4,512]{2,0,1:T(8,128)(2,1)S(1)} %bitcast.83), kind=kOutput, calls=%fused_computation.5 | convolution fusion | flops 2218917888 | bytes 7488000 | tf_op jit(solution)/shard_map/crp,hpq->rhcq/dot_general | solution.py:36
  13.2 7.2 %gather_fusion.1 = bf16[32,264,512]{2,1,0:T(8,128)(2,1)} fusion(bf16[16,264,512]{2,1,0:T(8,128)(2,1)} %bitcast.79, s32[1024]{0:T(1024)S(1)} %pad_clamp_fusion), kind=kCustom, calls=%fused_computation.1 | custom fusion | bytes 17301632 | tf_op jit(solution)/shard_map/jit(_take)/gather | solution.py:43
  20.4 104.8 %all_to_all.5 = bf16[16,528,512]{2,1,0:T(8,128)(2,1)S(1)} all-to-all(bf16[16,528,512]{2,1,0:T(8,128)(2,1)} %bitcast.78), channel_id=1, replica_groups=mesh['rcv'=16,'twin'=16] {'twin'}, dimensions={0} | all-to-all | bytes 17301504 | tf_op jit(solution)/shard_map/all_to_all | solution.py:49
  125.3 3.3 %copy-done.2 = bf16[16,528,512]{2,1,0:T(8,128)(2,1)} copy-done((bf16[16,528,512]{2,1,0:T(8,128)(2,1)}, bf16[16,528,512]{2,1,0:T(8,128)(2,1)S(1)}, u32[]{:S(2)}) %copy-start.2) | copy-done | bytes 8650776
  128.6 0.1 copy.39
  128.7 1.1 fusion.40
  129.9 0.1 copy.30
  130.0 0.1 and.115
  130.2 0.1 eq.120
  130.2 0.9 fusion.16
  131.1 0.9 fusion.15
  132.0 4.3 %collective-permute-start.1 = (bf16[1,8,512]{2,1,0:T(8,128)(2,1)S(1)}, bf16[1,8,512]{2,1,0:T(8,128)(2,1)S(1)}, u32[]{:S(2)}, u32[]{:S(2)}) collective-permute-start(bf16[1,8,512]{2,1,0:T(8,128)(2,1)S(1)} %fusion.15), channel_id=1, source_target_pairs={{16,0},{32,16},{48,32},{64,48},{80,64},{96,80},{112,96},{128,112},... | collective-permute-start | bytes 24584 | tf_op jit(solution)/shard_map/ppermute | solution.py:80
  136.3 4.7 %collective-permute-start = (bf16[1,8,512]{2,1,0:T(8,128)(2,1)S(1)}, bf16[1,8,512]{2,1,0:T(8,128)(2,1)S(1)}, u32[]{:S(2)}, u32[]{:S(2)}) collective-permute-start(bf16[1,8,512]{2,1,0:T(8,128)(2,1)S(1)} %fusion.16), channel_id=1, source_target_pairs={{0,16},{16,32},{32,48},{48,64},{64,80},{80,96},{96,112},{112,128},... | collective-permute-start | bytes 24584 | tf_op jit(solution)/shard_map/ppermute | solution.py:79
  141.1 4.6 %fusion.7 = f32[33,8,8,512]{3,2,1,0:T(8,128)S(1)} fusion(bf16[32,33,8,512,1]{3,2,1,0,4:T(8,128)(2,1)} %bitcast.82, pred[8,8]{1,0:T(8,128)(4,1)S(1)} %bitcast.85, bf16[8,32]{0,1:T(8,128)(2,1)S(1)} %fusion.25), kind=kOutput, calls=%fused_computation.13 | convolution fusion | flops 553664512 | bytes 12976704 | tf_op jit(solution)/shard_map/irjk,jbkq->birq/dot_general | solution.py:64
  145.7 0.5 slice.61
  146.2 1.1 copy-done.1
  147.3 0.8 fusion.6
  148.1 0.3 maximum_convert_fusion
  148.5 2.0 %fusion.5 = bf16[256,8,512]{2,1,0:T(8,128)(2,1)} fusion(f32[258,8,512]{2,1,0:T(8,128)S(1)} %maximum_convert_fusion), kind=kLoop, calls=%fused_computation.9 | loop fusion | flops 5242880 | bytes 14680064 | tf_op jit(solution)/shard_map/convert_element_type | solution.py:84
  (26 shorter events, 0.6 us)
Async XLA Ops:
  0.0 9.2 %copy-start = (bf16[4,512,512]{2,1,0:T(8,128)(2,1)S(1)}, bf16[4,512,512]{2,1,0:T(8,128)(2,1)}, u32[]{:S(2)}) copy-start(bf16[4,512,512]{2,1,0:T(8,128)(2,1)} %param.7) | copy-start | bytes 6291460
  125.2 3.3 %copy-start.2 = (bf16[16,528,512]{2,1,0:T(8,128)(2,1)}, bf16[16,528,512]{2,1,0:T(8,128)(2,1)S(1)}, u32[]{:S(2)}) copy-start(bf16[16,528,512]{2,1,0:T(8,128)(2,1)S(1)} %all_to_all.5) | copy-start | bytes 25952260
  132.0 16.1 %collective-permute-start.1 = (bf16[1,8,512]{2,1,0:T(8,128)(2,1)S(1)}, bf16[1,8,512]{2,1,0:T(8,128)(2,1)S(1)}, u32[]{:S(2)}, u32[]{:S(2)}) collective-permute-start(bf16[1,8,512]{2,1,0:T(8,128)(2,1)S(1)} %fusion.15), channel_id=1, source_target_pairs={{16,0},{32,16},{48,32},{64,48},{80,64},{96,80},{112,96},{128,112},... | collective-permute-start | bytes 24584 | tf_op jit(solution)/shard_map/ppermute | solution.py:80
  136.3 11.8 %collective-permute-start = (bf16[1,8,512]{2,1,0:T(8,128)(2,1)S(1)}, bf16[1,8,512]{2,1,0:T(8,128)(2,1)S(1)}, u32[]{:S(2)}, u32[]{:S(2)}) collective-permute-start(bf16[1,8,512]{2,1,0:T(8,128)(2,1)S(1)} %fusion.16), channel_id=1, source_target_pairs={{0,16},{16,32},{32,48},{48,64},{64,80},{80,96},{96,112},{112,128},... | collective-permute-start | bytes 24584 | tf_op jit(solution)/shard_map/ppermute | solution.py:79
  145.7 1.6 %copy-start.1 = (bf16[256,8,512]{2,1,0:T(8,128)(2,1)S(1)}, bf16[256,8,512]{2,1,0:T(8,128)(2,1)}, u32[]{:S(2)}) copy-start(bf16[256,8,512]{2,1,0:T(8,128)(2,1)} %param.4) | copy-start | bytes 6291460

commit v11 on v6

--- a/solution.py
+++ b/solution.py
@@ -25,6 +25,12 @@
     pair_total = rec_count * order_count
     slot_count = pair_total // twin_count + 1
 
+    count = lax.axis_size("rcv")
+    forward = [(i, i + 1) for i in range(count - 1)]
+    backward = [(target, source) for source, target in forward]
+    prev_last = lax.ppermute(record[channels - 1], "rcv", forward)
+    next_first = lax.ppermute(record[0], "rcv", backward)
+
     guides = jnp.take(record, slip_block // twin_count, axis=1, mode="clip")
     estimates = jnp.einsum(
         "crp,hpq->rhcq", guides, order_ops, preferred_element_type=jnp.float32
@@ -33,7 +39,14 @@
 
     owner, slot, land_round = pair_routes(slip_block, ghost_lag, twin_count)
     meta_rows = 8
-    meta = jnp.broadcast_to(land_round.astype(jnp.bfloat16)[:, None, None], (pair_total, meta_rows, samples))
+    round_row = jnp.broadcast_to(land_round.astype(jnp.bfloat16)[:, None, None], (pair_total, 1, samples))
+    edge_guides = jnp.take(jnp.stack([prev_last, next_first]), slip_block // twin_count, axis=1, mode="clip")
+    edge_estimates = jnp.einsum(
+        "erp,hpq->rheq", edge_guides, order_ops, preferred_element_type=jnp.float32
+    ).astype(jnp.bfloat16).reshape(pair_total, 2, samples)
+    meta = jnp.concatenate(
+        [round_row, edge_estimates, jnp.zeros((pair_total, meta_rows - 3, samples), jnp.bfloat16)], axis=1
+    )
     blank = jnp.zeros((1, channels + meta_rows, samples), jnp.bfloat16)
     tagged = jnp.concatenate([jnp.concatenate([estimates, meta], axis=1), blank], axis=0)
     chosen = (owner[:, None, None] == jnp.arange(twin_count, dtype=jnp.int32)[None, :, None]) & (
@@ -44,7 +57,7 @@
     outgoing = outgoing.reshape(twin_count, slot_count * (channels + meta_rows), samples)
     sub = 8
     same = lax.broadcasted_iota(jnp.int32, (sub, 1, 1, sub), 0) == lax.broadcasted_iota(jnp.int32, (sub, 1, 1, sub), 3)
-    outgoing, same = lax.optimization_barrier((outgoing, same))
+    outgoing, same, prev_last, next_first = lax.optimization_barrier((outgoing, same, prev_last, next_first))
     arrived = lax.all_to_all(outgoing, "twin", split_axis=0, concat_axis=0, tiled=True)
     arrived = arrived.reshape(twin_count, slot_count, channels + meta_rows, samples)
 
@@ -61,11 +74,14 @@
     def cleaned_rows(lo, hi):
         return (record[lo:hi].astype(jnp.float32) - noise[lo:hi]).astype(jnp.bfloat16)
 
-    count = lax.axis_size("rcv")
-    forward = [(i, i + 1) for i in range(count - 1)]
-    backward = [(target, source) for source, target in forward]
-    low = lax.ppermute(cleaned_rows(channels - 1, channels), "rcv", forward)
-    high = lax.ppermute(cleaned_rows(0, 1), "rcv", backward)
+    def halo_row(row, neighbour):
+        edge_noise = jnp.einsum(
+            "nsr,nsq->rq", hit, arrived[:, :, row], preferred_element_type=jnp.float32
+        )
+        return (neighbour.astype(jnp.float32) - edge_noise).astype(jnp.bfloat16)[None]
+
+    low = halo_row(channels + 1, prev_last)
+    high = halo_row(channels + 2, next_first)
     cleaned = cleaned_rows(0, channels)
     widened = jnp.concatenate([low, cleaned, high], axis=0).astype(jnp.float32)
     smooth = 0.5 * widened[1:-1] + 0.25 * (widened[:-2] + widened[2:])

time: 151 us -> 154 us (1.020)
  local copies, waits for them, and re-layouts: 16.7 us -> 21.7 us
  waiting for transfers between devices: 3 us -> 0.01 us
  matrix products: 7.12 us -> 9.69 us
  starting transfers between devices: 8.96 us -> 7.23 us
    ppermute x2, waiting for transfers between devices: 3 us -> 0.01 us  [the longest x1 0.01 us: local(): next_first = lax.ppermute(record[0], 'rcv', backward)]
    concatenate x0 -> x2, local copies, waits for them, and re-layouts: none -> 2.52 us  [the longest x1 2.44 us: local(): jnp.concatenate([jnp.concatenate([estimates, meta], axis=1), blank], axis=0)]
    dot_general x1, matrix products: 2.34 us -> 4.27 us  [local(): jnp.einsum('crp,hpq->rhcq', guides, order_ops, preferred_element_type=jnp...]
    ppermute x2, starting transfers between devices: 8.96 us -> 7.23 us  [the longest x1 5.3 us: local(): prev_last = lax.ppermute(record[channels - 1], 'rcv', forward)]
  transfers between devices with their start and end apart: 2 -> 2, of which waited for: 1 -> 0; matrix products, arithmetic and copies ran while one was open for 1% -> 9% of each run, Pallas kernels for 0% -> 0%
where the time goes in v11:
time: 154 us
  blocking collectives  105 us (68%)
  local copies, waits for them, and re-layouts  21.7 us (14%)
  other arithmetic  9.88 us (6%)
  matrix products  9.69 us (6%)
  starting transfers between devices  7.23 us (5%)
    all_to_all x1, blocking collectives, local(): lax.all_to_all(outgoing, 'twin', split_axis=0, concat_axis=0, tiled=True)  105 us
    gather x1, local copies, waits for them, and re-layouts, local(): jnp.take(tagged, pick.reshape(twin_count * slot_count), axis=0, mode='clip')  7.26 us
    gather x1, local copies, waits for them, and re-layouts, local(): guides = jnp.take(record, slip_block // twin_count, axis=1, mode='clip')  5.35 us
    ppermute x1, starting transfers between devices, local(): prev_last = lax.ppermute(record[channels - 1], 'rcv', forward)  5.3 us
    dot_general x1, matrix products, local(): jnp.einsum('irjk,jbkq->birq', spread, stacked, preferred_element_type=jnp...  4.65 us
    dot_general x1, matrix products, local(): jnp.einsum('crp,hpq->rhcq', guides, order_ops, preferred_element_type=jnp...  4.27 us
    unnamed x6, local copies, waits for them, and re-layouts  3.75 us
  transfers between devices with their start and end apart: 2, of which 0 were waited for; matrix products, arithmetic and copies ran while one was open for 9% of the time, Pallas kernels for 0%

profile of v11, /device:TPU:97, one launch (start us, length us, event | category | flops | bytes accessed | tf_op | source)
XLA Modules:
  0.0 153.9 jit_solution(11653081425434179895)
XLA Ops:
  0.0 0.9 slice_bitcast_fusion.1
  0.9 5.3 %collective-permute-start = (bf16[8,512]{1,0:T(8,128)(2,1)S(1)}, bf16[8,512]{1,0:T(8,128)(2,1)S(1)}, u32[]{:S(2)}, u32[]{:S(2)}) collective-permute-start(bf16[8,512]{1,0:T(8,128)(2,1)S(1)} %get-tuple-element.17), channel_id=1, source_target_pairs={{0,16},{16,32},{32,48},{48,64},{64,80},{80,96},{96,112},{112,128},... | collective-permute-start | bytes 24584 | tf_op jit(solution)/shard_map/ppermute | solution.py:31
  6.2 1.9 %collective-permute-start.1 = (bf16[8,512]{1,0:T(8,128)(2,1)S(1)}, bf16[8,512]{1,0:T(8,128)(2,1)S(1)}, u32[]{:S(2)}, u32[]{:S(2)}) collective-permute-start(bf16[8,512]{1,0:T(8,128)(2,1)S(1)} %get-tuple-element.18), channel_id=1, source_target_pairs={{16,0},{32,16},{48,32},{64,48},{80,64},{96,80},{112,96},{128,112},... | collective-permute-start | bytes 24584 | tf_op jit(solution)/shard_map/ppermute | solution.py:32
  8.1 0.7 and_select_fusion.2
  8.8 0.8 subtract_compare_fusion
  9.5 0.8 fusion.32
  10.3 0.1 ge.19
  10.4 0.1 ne.73
  10.6 0.2 convert_reduce_fusion
  10.9 0.1 and_reduce_fusion.1
  11.0 0.6 and_reduce_fusion
  11.7 0.1 reshape.186
  11.8 5.3 %gather_fusion = bf16[4,256,512]{2,0,1:T(4,128)(2,1)S(1)} fusion(bf16[256,8,512]{2,1,0:T(8,128)(2,1)} %param.4, s32[1024]{0:T(1024)S(1)} %pad_clamp_fusion.1), kind=kCustom, calls=%fused_computation | custom fusion | bytes 2097168 | tf_op jit(solution)/shard_map/jit(_take)/gather | solution.py:34
  17.2 4.3 %convolution_convert_fusion = bf16[256,4,4,512]{3,0,2,1:T(8,128)(2,1)} fusion(bf16[4,512,512]{2,1,0:T(8,128)(2,1)S(1)} %copy-done, bf16[256,4,512,1]{2,1,0,3:T(4,128)(2,1)S(1)} %bitcast.66), kind=kOutput, calls=%fused_computation.13 | convolution fusion | flops 2149580800 | bytes 7340032 | tf_op jit(solution)/shard_map/crp,hpq->rhcq/dot_general | solution.py:35
  21.6 0.6 gather_fusion.1
  22.1 0.4 fusion.15
  22.7 2.9 %maximum_maximum_fusion = bf16[16,264,512]{2,1,0:T(8,128)(2,1)S(1)} fusion(bf16[16,2,512]{2,1,0:T(2,128)(2,1)S(1)} %bitcast.67, bf16[16,1,512]{2,1,0:T(2,128)(2,1)S(1)} %broadcast_in_dim.67, bf16[16,256,512]{2,1,0:T(8,128)(2,1)} %bitcast.65, bf16[264]{0:T(512)(128)(2,1)S(1)} %pad.7.clone), kind=kLoop, calls=%fused_computation.5 | loop fusion | flops 17301504 | bytes 8569360 | tf_op jit(solution)/shard_map/concatenate | solution.py:51
  25.5 2.4 %concatenate.10 = bf16[17,264,512]{2,1,0:T(8,128)(2,1)} pad(bf16[16,264,512]{2,1,0:T(8,128)(2,1)S(1)} %maximum_maximum_fusion, bf16[]{:T(256)} %constant.60.clone.1), padding=0_1x0_0x0_0 | pad | bytes 8921090 | tf_op jit(solution)/shard_map/concatenate | solution.py:51
  28.0 7.3 %gather_fusion.2 = bf16[32,264,512]{2,1,0:T(8,128)(2,1)} fusion(bf16[17,264,512]{2,1,0:T(8,128)(2,1)} %concatenate.10, s32[1024]{0:T(1024)S(1)} %pad_clamp_fusion), kind=kCustom, calls=%fused_computation.2 | custom fusion | bytes 17301632 | tf_op jit(solution)/shard_map/jit(_take)/gather | solution.py:56
  35.2 105.2 %all_to_all.5 = bf16[16,528,512]{2,1,0:T(8,128)(2,1)S(1)} all-to-all(bf16[16,528,512]{2,1,0:T(8,128)(2,1)} %bitcast.60), channel_id=1, replica_groups=mesh['rcv'=16,'twin'=16] {'twin'}, dimensions={0} | all-to-all | bytes 17301504 | tf_op jit(solution)/shard_map/all_to_all | solution.py:61
  140.5 0.6 fusion.36
  141.1 2.6 %copy-done.2 = bf16[16,528,512]{2,1,0:T(8,128)(2,1)} copy-done((bf16[16,528,512]{2,1,0:T(8,128)(2,1)}, bf16[16,528,512]{2,1,0:T(8,128)(2,1)S(1)}, u32[]{:S(2)}) %copy-start.2) | copy-done | bytes 8650776
  143.8 0.1 fusion.37
  144.0 0.1 copy.20
  144.1 0.2 convolution_bitcast_fusion.1
  144.3 0.2 convolution_bitcast_fusion
  144.5 4.6 %fusion.6 = f32[33,8,8,512]{3,2,1,0:T(8,128)S(1)} fusion(bf16[32,33,8,512,1]{3,2,1,0,4:T(8,128)(2,1)} %bitcast.64, pred[8,8]{1,0:T(8,128)(4,1)S(1)} %bitcast.73, bf16[8,32]{0,1:T(8,128)(2,1)S(1)} %fusion.24), kind=kOutput, calls=%fused_computation.14 | convolution fusion | flops 553664512 | bytes 12976704 | tf_op jit(solution)/shard_map/irjk,jbkq->birq/dot_general | solution.py:71
  149.2 0.5 slice.48
  149.6 1.1 copy-done.1
  150.8 0.8 fusion.5
  151.6 0.3 maximum_convert_fusion
  151.9 2.0 %fusion.4 = bf16[256,8,512]{2,1,0:T(8,128)(2,1)} fusion(f32[258,8,512]{2,1,0:T(8,128)S(1)} %maximum_convert_fusion), kind=kLoop, calls=%fused_computation.9 | loop fusion | flops 5242880 | bytes 14680064 | tf_op jit(solution)/shard_map/convert_element_type | solution.py:88
  (26 shorter events, 0.8 us)
Async XLA Ops:
  0.0 17.2 %copy-start = (bf16[4,512,512]{2,1,0:T(8,128)(2,1)S(1)}, bf16[4,512,512]{2,1,0:T(8,128)(2,1)}, u32[]{:S(2)}) copy-start(bf16[4,512,512]{2,1,0:T(8,128)(2,1)} %param.7) | copy-start | bytes 6291460
  0.9 20.7 %collective-permute-start = (bf16[8,512]{1,0:T(8,128)(2,1)S(1)}, bf16[8,512]{1,0:T(8,128)(2,1)S(1)}, u32[]{:S(2)}, u32[]{:S(2)}) collective-permute-start(bf16[8,512]{1,0:T(8,128)(2,1)S(1)} %get-tuple-element.17), channel_id=1, source_target_pairs={{0,16},{16,32},{32,48},{48,64},{64,80},{80,96},{96,112},{112,128},... | collective-permute-start | bytes 24584 | tf_op jit(solution)/shard_map/ppermute | solution.py:31
  6.2 15.4 %collective-permute-start.1 = (bf16[8,512]{1,0:T(8,128)(2,1)S(1)}, bf16[8,512]{1,0:T(8,128)(2,1)S(1)}, u32[]{:S(2)}, u32[]{:S(2)}) collective-permute-start(bf16[8,512]{1,0:T(8,128)(2,1)S(1)} %get-tuple-element.18), channel_id=1, source_target_pairs={{16,0},{32,16},{48,32},{64,48},{80,64},{96,80},{112,96},{128,112},... | collective-permute-start | bytes 24584 | tf_op jit(solution)/shard_map/ppermute | solution.py:32
  140.5 3.3 %copy-start.2 = (bf16[16,528,512]{2,1,0:T(8,128)(2,1)}, bf16[16,528,512]{2,1,0:T(8,128)(2,1)S(1)}, u32[]{:S(2)}) copy-start(bf16[16,528,512]{2,1,0:T(8,128)(2,1)S(1)} %all_to_all.5) | copy-start | bytes 25952260
  149.2 1.6 %copy-start.1 = (bf16[256,8,512]{2,1,0:T(8,128)(2,1)S(1)}, bf16[256,8,512]{2,1,0:T(8,128)(2,1)}, u32[]{:S(2)}) copy-start(bf16[256,8,512]{2,1,0:T(8,128)(2,1)} %param.4) | copy-start | bytes 6291460

commit v12 on v11

--- a/solution.py
+++ b/solution.py
@@ -39,30 +39,37 @@
 
     owner, slot, land_round = pair_routes(slip_block, ghost_lag, twin_count)
     meta_rows = 8
-    round_row = jnp.broadcast_to(land_round.astype(jnp.bfloat16)[:, None, None], (pair_total, 1, samples))
+    tag_rows = jnp.broadcast_to(
+        jnp.stack([land_round, owner, slot], axis=1).astype(jnp.bfloat16)[:, :, None], (pair_total, 3, samples)
+    )
     edge_guides = jnp.take(jnp.stack([prev_last, next_first]), slip_block // twin_count, axis=1, mode="clip")
     edge_estimates = jnp.einsum(
         "erp,hpq->rheq", edge_guides, order_ops, preferred_element_type=jnp.float32
     ).astype(jnp.bfloat16).reshape(pair_total, 2, samples)
     meta = jnp.concatenate(
-        [round_row, edge_estimates, jnp.zeros((pair_total, meta_rows - 3, samples), jnp.bfloat16)], axis=1
+        [tag_rows, edge_estimates, jnp.zeros((pair_total, meta_rows - 5, samples), jnp.bfloat16)], axis=1
     )
-    blank = jnp.zeros((1, channels + meta_rows, samples), jnp.bfloat16)
-    tagged = jnp.concatenate([jnp.concatenate([estimates, meta], axis=1), blank], axis=0)
+    tagged = jnp.concatenate([estimates, meta], axis=1)
     chosen = (owner[:, None, None] == jnp.arange(twin_count, dtype=jnp.int32)[None, :, None]) & (
         slot[:, None, None] == jnp.arange(slot_count, dtype=jnp.int32)[None, None, :]
     )
-    pick = jnp.where(jnp.any(chosen, axis=0), jnp.argmax(chosen, axis=0), pair_total)
+    pick = jnp.argmax(chosen, axis=0)
     outgoing = jnp.take(tagged, pick.reshape(twin_count * slot_count), axis=0, mode="clip")
     outgoing = outgoing.reshape(twin_count, slot_count * (channels + meta_rows), samples)
     sub = 8
     same = lax.broadcasted_iota(jnp.int32, (sub, 1, 1, sub), 0) == lax.broadcasted_iota(jnp.int32, (sub, 1, 1, sub), 3)
-    outgoing, same, prev_last, next_first = lax.optimization_barrier((outgoing, same, prev_last, next_first))
+    me = lax.axis_index("twin")
+    outgoing, same, me, prev_last, next_first = lax.optimization_barrier((outgoing, same, me, prev_last, next_first))
     arrived = lax.all_to_all(outgoing, "twin", split_axis=0, concat_axis=0, tiled=True)
     arrived = arrived.reshape(twin_count, slot_count, channels + meta_rows, samples)
 
-    arrived_rounds = arrived[:, :, channels, 0].astype(jnp.int32)
-    hit = (arrived_rounds[:, :, None] == jnp.arange(rounds, dtype=jnp.int32)[None, None, :]).astype(jnp.bfloat16)
+    arrived_tags = arrived[:, :, channels : channels + 3, 0].astype(jnp.int32)
+    kept = (arrived_tags[:, :, 1] == me) & (
+        arrived_tags[:, :, 2] == jnp.arange(slot_count, dtype=jnp.int32)[None, :]
+    )
+    hit = (
+        kept[:, :, None] & (arrived_tags[:, :, 0][:, :, None] == jnp.arange(rounds, dtype=jnp.int32)[None, None, :])
+    ).astype(jnp.bfloat16)
 
     sub = 8
     blocks = (channels + meta_rows) // sub
@@ -80,8 +87,8 @@
         )
         return (neighbour.astype(jnp.float32) - edge_noise).astype(jnp.bfloat16)[None]
 
-    low = halo_row(channels + 1, prev_last)
-    high = halo_row(channels + 2, next_first)
+    low = halo_row(channels + 3, prev_last)
+    high = halo_row(channels + 4, next_first)
     cleaned = cleaned_rows(0, channels)
     widened = jnp.concatenate([low, cleaned, high], axis=0).astype(jnp.float32)
     smooth = 0.5 * widened[1:-1] + 0.25 * (widened[:-2] + widened[2:])

time: 154 us -> 154 us (level)
    concatenate x2 -> x1, local copies, waits for them, and re-layouts: 2.52 us -> 0.08 us  [local(): tagged = jnp.concatenate([estimates, meta], axis=1)]
    unnamed x6 -> x7, local copies, waits for them, and re-layouts: 3.75 us -> 4.56 us
where the time goes in v12:
time: 154 us
  blocking collectives  105 us (68%)
  local copies, waits for them, and re-layouts  21.1 us (14%)
  other arithmetic  10.5 us (7%)
  matrix products  9.7 us (6%)
  starting transfers between devices  7.23 us (5%)
    all_to_all x1, blocking collectives, local(): lax.all_to_all(outgoing, 'twin', split_axis=0, concat_axis=0, tiled=True)  105 us
    gather x1, local copies, waits for them, and re-layouts, local(): jnp.take(tagged, pick.reshape(twin_count * slot_count), axis=0, mode='clip')  7.22 us
    ppermute x1, starting transfers between devices, local(): prev_last = lax.ppermute(record[channels - 1], 'rcv', forward)  5.3 us
    gather x1, local copies, waits for them, and re-layouts, local(): guides = jnp.take(record, slip_block // twin_count, axis=1, mode='clip')  4.88 us
    dot_general x1, matrix products, local(): jnp.einsum('irjk,jbkq->birq', spread, stacked, preferred_element_type=jnp...  4.65 us
    unnamed x7, local copies, waits for them, and re-layouts  4.56 us
    dot_general x1, matrix products, local(): jnp.einsum('crp,hpq->rhcq', guides, order_ops, preferred_element_type=jnp...  4.28 us
    concatenate x1, other arithmetic, local(): tagged = jnp.concatenate([estimates, meta], axis=1)  4.22 us
  transfers between devices with their start and end apart: 2, of which 0 were waited for; matrix products, arithmetic and copies ran while one was open for 9% of the time, Pallas kernels for 0%

profile of v12, /device:TPU:97, one launch (start us, length us, event | category | flops | bytes accessed | tf_op | source)
XLA Modules:
  0.0 154.0 jit_solution(6611383579340523002)
XLA Ops:
  0.0 0.9 slice_bitcast_fusion.1
  0.9 5.3 %collective-permute-start = (bf16[8,512]{1,0:T(8,128)(2,1)S(1)}, bf16[8,512]{1,0:T(8,128)(2,1)S(1)}, u32[]{:S(2)}, u32[]{:S(2)}) collective-permute-start(bf16[8,512]{1,0:T(8,128)(2,1)S(1)} %get-tuple-element.19), channel_id=1, source_target_pairs={{0,16},{16,32},{32,48},{48,64},{64,80},{80,96},{96,112},{112,128},... | collective-permute-start | bytes 24584 | tf_op jit(solution)/shard_map/ppermute | solution.py:31
  6.2 1.9 %collective-permute-start.1 = (bf16[8,512]{1,0:T(8,128)(2,1)S(1)}, bf16[8,512]{1,0:T(8,128)(2,1)S(1)}, u32[]{:S(2)}, u32[]{:S(2)}) collective-permute-start(bf16[8,512]{1,0:T(8,128)(2,1)S(1)} %get-tuple-element.20), channel_id=1, source_target_pairs={{16,0},{32,16},{48,32},{64,48},{80,64},{96,80},{112,96},{128,112},... | collective-permute-start | bytes 24584 | tf_op jit(solution)/shard_map/ppermute | solution.py:32
  8.1 0.7 and_select_fusion.3
  8.8 0.8 sign_compare_fusion
  9.7 0.8 fusion.37
  10.6 0.2 convert_reduce_fusion
  10.9 0.1 ne.95
  11.1 0.6 iota_reduce_fusion
  11.8 0.1 reshape.250
  11.9 4.9 %gather_fusion = bf16[4,256,512]{2,0,1:T(4,128)(2,1)S(1)} fusion(bf16[256,8,512]{2,1,0:T(8,128)(2,1)} %param.4, s32[1024]{0:T(1024)S(1)} %pad_clamp_fusion.1), kind=kCustom, calls=%fused_computation | custom fusion | bytes 2097168 | tf_op jit(solution)/shard_map/jit(_take)/gather | solution.py:34
  16.8 4.3 %convolution_convert_fusion = bf16[256,4,4,512]{3,0,2,1:T(8,128)(2,1)} fusion(bf16[4,512,512]{2,1,0:T(8,128)(2,1)S(1)} %copy-done, bf16[256,4,512,1]{2,1,0,3:T(4,128)(2,1)S(1)} %bitcast.81), kind=kOutput, calls=%fused_computation.13 | convolution fusion | flops 2149580800 | bytes 7340032 | tf_op jit(solution)/shard_map/crp,hpq->rhcq/dot_general | solution.py:35
  21.1 0.1 copy.33
  21.3 0.6 gather_fusion.1
  21.9 0.4 fusion.15
  22.4 4.2 %maximum_maximum_fusion = bf16[16,264,512]{2,1,0:T(8,128)(2,1)} fusion(bf16[16,2,512]{2,1,0:T(2,128)(2,1)S(1)} %bitcast.82, bf16[16,3,512]{2,1,0:T(4,128)(2,1)S(1)} %broadcast_in_dim.66, bf16[16,256,512]{2,1,0:T(8,128)(2,1)} %bitcast.80, bf16[264]{0:T(512)(128)(2,1)S(1)} %pad.6.clone), kind=kLoop, calls=%fused_computation.5 | loop fusion | flops 17301504 | bytes 8602128 | tf_op jit(solution)/shard_map/concatenate | solution.py:52
  26.6 7.2 %gather_fusion.2 = bf16[32,264,512]{2,1,0:T(8,128)(2,1)} fusion(bf16[16,264,512]{2,1,0:T(8,128)(2,1)} %maximum_maximum_fusion, s32[1024]{0:T(1024)S(1)} %pad_clamp_fusion), kind=kCustom, calls=%fused_computation.2 | custom fusion | bytes 17301632 | tf_op jit(solution)/shard_map/jit(_take)/gather | solution.py:57
  33.9 105.3 %all_to_all.5 = bf16[16,528,512]{2,1,0:T(8,128)(2,1)S(1)} all-to-all(bf16[16,528,512]{2,1,0:T(8,128)(2,1)} %bitcast.76), channel_id=1, replica_groups=mesh['rcv'=16,'twin'=16] {'twin'}, dimensions={0} | all-to-all | bytes 17301504 | tf_op jit(solution)/shard_map/all_to_all | solution.py:63
  139.2 3.3 %copy-done.2 = bf16[16,528,512]{2,1,0:T(8,128)(2,1)} copy-done((bf16[16,528,512]{2,1,0:T(8,128)(2,1)}, bf16[16,528,512]{2,1,0:T(8,128)(2,1)S(1)}, u32[]{:S(2)}) %copy-start.2) | copy-done | bytes 8650776
  142.5 0.1 copy.54
  142.6 1.2 fusion.44
  143.8 0.1 copy.40
  143.9 0.1 and.124
  144.1 0.1 eq.120
  144.3 4.7 %fusion.6 = f32[33,8,8,512]{3,2,1,0:T(8,128)S(1)} fusion(bf16[32,33,8,512,1]{3,2,1,0,4:T(8,128)(2,1)} %bitcast.79, pred[8,8]{1,0:T(8,128)(4,1)S(1)} %bitcast.86, bf16[8,32]{0,1:T(8,128)(2,1)S(1)} %fusion.25), kind=kOutput, calls=%fused_computation.14 | convolution fusion | flops 553664512 | bytes 12976704 | tf_op jit(solution)/shard_map/irjk,jbkq->birq/dot_general | solution.py:78
  148.9 0.5 slice.63
  149.4 1.1 copy-done.1
  150.5 0.8 fusion.5
  151.3 0.2 convolution_bitcast_fusion
  151.5 0.2 fusion.26
  151.7 0.3 maximum_convert_fusion
  152.0 2.0 %fusion.4 = bf16[256,8,512]{2,1,0:T(8,128)(2,1)} fusion(f32[258,8,512]{2,1,0:T(8,128)S(1)} %maximum_convert_fusion), kind=kLoop, calls=%fused_computation.9 | loop fusion | flops 5242880 | bytes 14680064 | tf_op jit(solution)/shard_map/convert_element_type | solution.py:95
  (34 shorter events, 1.1 us)
Async XLA Ops:
  0.0 16.8 %copy-start = (bf16[4,512,512]{2,1,0:T(8,128)(2,1)S(1)}, bf16[4,512,512]{2,1,0:T(8,128)(2,1)}, u32[]{:S(2)}) copy-start(bf16[4,512,512]{2,1,0:T(8,128)(2,1)} %param.7) | copy-start | bytes 6291460
  0.9 20.4 %collective-permute-start = (bf16[8,512]{1,0:T(8,128)(2,1)S(1)}, bf16[8,512]{1,0:T(8,128)(2,1)S(1)}, u32[]{:S(2)}, u32[]{:S(2)}) collective-permute-start(bf16[8,512]{1,0:T(8,128)(2,1)S(1)} %get-tuple-element.19), channel_id=1, source_target_pairs={{0,16},{16,32},{32,48},{48,64},{64,80},{80,96},{96,112},{112,128},... | collective-permute-start | bytes 24584 | tf_op jit(solution)/shard_map/ppermute | solution.py:31
  6.2 15.1 %collective-permute-start.1 = (bf16[8,512]{1,0:T(8,128)(2,1)S(1)}, bf16[8,512]{1,0:T(8,128)(2,1)S(1)}, u32[]{:S(2)}, u32[]{:S(2)}) collective-permute-start(bf16[8,512]{1,0:T(8,128)(2,1)S(1)} %get-tuple-element.20), channel_id=1, source_target_pairs={{16,0},{32,16},{48,32},{64,48},{80,64},{96,80},{112,96},{128,112},... | collective-permute-start | bytes 24584 | tf_op jit(solution)/shard_map/ppermute | solution.py:32
  139.1 3.3 %copy-start.2 = (bf16[16,528,512]{2,1,0:T(8,128)(2,1)}, bf16[16,528,512]{2,1,0:T(8,128)(2,1)S(1)}, u32[]{:S(2)}) copy-start(bf16[16,528,512]{2,1,0:T(8,128)(2,1)S(1)} %all_to_all.5) | copy-start | bytes 25952260
  148.9 1.6 %copy-start.1 = (bf16[256,8,512]{2,1,0:T(8,128)(2,1)S(1)}, bf16[256,8,512]{2,1,0:T(8,128)(2,1)}, u32[]{:S(2)}) copy-start(bf16[256,8,512]{2,1,0:T(8,128)(2,1)} %param.4) | copy-start | bytes 6291460

commit v13 on v7

--- a/solution.py
+++ b/solution.py
@@ -21,6 +21,8 @@
 def local(record, slip_block, ghost_lag, order_ops):
     twin_count = lax.axis_size("twin")
     channels, rounds, samples = record.shape
+    table = lax.optimization_barrier(jnp.concatenate([slip_block[:, None], ghost_lag], axis=1))
+    slip_block, ghost_lag = table[:, 0], table[:, 1:]
     rec_count, order_count = ghost_lag.shape
     pair_total = rec_count * order_count
     slot_count = pair_total // twin_count + 1

time: 150 us -> 150 us (level)
  no operation moved by 1% of the time
where the time goes in v13:
time: 150 us; the launch traced here: 149 us
  blocking collectives  105 us (70%)
  local copies, waits for them, and re-layouts  18.5 us (12%)
  starting transfers between devices  8.99 us (6%)
  matrix products  8.77 us (6%)
  other arithmetic  8.2 us (5%)
    all_to_all x1, blocking collectives, local(): lax.all_to_all(outgoing, 'twin', split_axis=0, concat_axis=0, tiled=True)  105 us
    gather x1, local copies, waits for them, and re-layouts, local(): jnp.take(tagged, pick.reshape(twin_count * slot_count), axis=0, mode='clip')  7.3 us
    gather x1, local copies, waits for them, and re-layouts, local(): guides = jnp.take(record, slip_block // twin_count, axis=1, mode='clip')  5.26 us
    ppermute x1, starting transfers between devices, local(): low = lax.ppermute(edge_row(channels - 1), 'rcv', forward)  4.66 us
    dot_general x1, matrix products, local(): jnp.einsum('irjk,jbkq->birq', spread, stacked, preferred_element_type=jnp...  4.65 us
    ppermute x1, starting transfers between devices, local(): high = lax.ppermute(edge_row(0), 'rcv', backward)  4.32 us
    unnamed x6, local copies, waits for them, and re-layouts  3.75 us
  transfers between devices with their start and end apart: 2, of which 0 were waited for; matrix products, arithmetic and copies ran while one was open for 4% of the time, Pallas kernels for 0%

profile of v13, /device:TPU:97, one launch (start us, length us, event | category | flops | bytes accessed | tf_op | source)
XLA Modules:
  0.0 149.2 jit_solution(2294022751452711425)
XLA Ops:
  0.0 0.9 copy.14
  0.9 0.8 pad_add_fusion
  1.7 0.2 fusion.30
  2.0 0.1 ge.19
  2.1 0.1 ne.72
  2.1 0.1 rem.46
  2.2 0.1 div.28
  2.3 0.2 convert_reduce_fusion
  2.6 0.1 and_reduce_fusion.1
  2.7 0.6 and_reduce_fusion
  3.3 0.1 copy.16
  3.4 0.1 reshape.177
  3.5 5.3 %gather_fusion = bf16[4,256,512]{2,0,1:T(4,128)(2,1)S(1)} fusion(bf16[256,8,512]{2,1,0:T(8,128)(2,1)} %param.4, s32[1024]{0:T(1024)S(1)} %pad_clamp_fusion.1), kind=kCustom, calls=%fused_computation | custom fusion | bytes 2097168 | tf_op jit(solution)/shard_map/jit(_take)/gather | solution.py:30
  8.8 2.3 %convolution_convert_fusion = bf16[256,4,4,512]{3,0,2,1:T(8,128)(2,1)S(1)} fusion(bf16[4,512,512]{2,1,0:T(8,128)(2,1)S(1)} %copy-done, bf16[256,4,512,1]{2,1,0,3:T(4,128)(2,1)S(1)} %bitcast.67), kind=kOutput, calls=%fused_computation.15 | convolution fusion | flops 2149580800 | bytes 7340032 | tf_op jit(solution)/shard_map/crp,hpq->rhcq/dot_general | solution.py:31
  11.2 2.3 %fusion.4 = bf16[17,264,512]{2,1,0:T(8,128)(2,1)} fusion(bf16[16,8,512]{2,1,0:T(8,128)(2,1)S(1)} %broadcast_in_dim.62, bf16[16,256,512]{2,1,0:T(8,128)(2,1)S(1)} %bitcast.66), kind=kLoop, calls=%fused_computation.7 | loop fusion | flops 16084992 | bytes 8921088 | tf_op jit(solution)/shard_map/concatenate | solution.py:40
  13.5 7.3 %gather_fusion.1 = bf16[32,264,512]{2,1,0:T(8,128)(2,1)} fusion(bf16[17,264,512]{2,1,0:T(8,128)(2,1)} %fusion.4, s32[1024]{0:T(1024)S(1)} %pad_clamp_fusion), kind=kCustom, calls=%fused_computation.1 | custom fusion | bytes 17301632 | tf_op jit(solution)/shard_map/jit(_take)/gather | solution.py:45
  20.8 104.6 %all_to_all.5 = bf16[16,528,512]{2,1,0:T(8,128)(2,1)S(1)} all-to-all(bf16[16,528,512]{2,1,0:T(8,128)(2,1)} %bitcast.61), channel_id=1, replica_groups=mesh['rcv'=16,'twin'=16] {'twin'}, dimensions={0} | all-to-all | bytes 17301504 | tf_op jit(solution)/shard_map/all_to_all | solution.py:50
  125.4 0.6 fusion.37
  126.1 2.6 %copy-done.2 = bf16[16,528,512]{2,1,0:T(8,128)(2,1)} copy-done((bf16[16,528,512]{2,1,0:T(8,128)(2,1)}, bf16[16,528,512]{2,1,0:T(8,128)(2,1)S(1)}, u32[]{:S(2)}) %copy-start.2) | copy-done | bytes 8650776
  128.7 0.1 fusion.38
  128.8 0.1 reshape.165
  129.0 0.1 copy.17
  129.1 0.9 fusion.18
  130.0 0.9 fusion.17
  130.8 4.3 %collective-permute-start.1 = (bf16[1,8,512]{2,1,0:T(8,128)(2,1)S(1)}, bf16[1,8,512]{2,1,0:T(8,128)(2,1)S(1)}, u32[]{:S(2)}, u32[]{:S(2)}) collective-permute-start(bf16[1,8,512]{2,1,0:T(8,128)(2,1)S(1)} %fusion.17), channel_id=1, source_target_pairs={{16,0},{32,16},{48,32},{64,48},{80,64},{96,80},{112,96},{128,112},... | collective-permute-start | bytes 24584 | tf_op jit(solution)/shard_map/ppermute | solution.py:76
  135.2 4.7 %collective-permute-start = (bf16[1,8,512]{2,1,0:T(8,128)(2,1)S(1)}, bf16[1,8,512]{2,1,0:T(8,128)(2,1)S(1)}, u32[]{:S(2)}, u32[]{:S(2)}) collective-permute-start(bf16[1,8,512]{2,1,0:T(8,128)(2,1)S(1)} %fusion.18), channel_id=1, source_target_pairs={{0,16},{16,32},{32,48},{48,64},{64,80},{80,96},{96,112},{112,128},... | collective-permute-start | bytes 24584 | tf_op jit(solution)/shard_map/ppermute | solution.py:75
  139.9 4.6 %fusion.9 = f32[33,8,8,512]{3,2,1,0:T(8,128)S(1)} fusion(bf16[32,33,8,512,1]{3,2,1,0,4:T(8,128)(2,1)} %bitcast.65, pred[8,8]{1,0:T(8,128)(4,1)S(1)} %bitcast.71, bf16[8,32]{0,1:T(8,128)(2,1)S(1)} %fusion.25), kind=kOutput, calls=%fused_computation.16 | convolution fusion | flops 553664512 | bytes 12976704 | tf_op jit(solution)/shard_map/irjk,jbkq->birq/dot_general | solution.py:60
  144.5 0.5 slice.54
  145.0 1.1 copy-done.1
  146.1 0.8 fusion.8
  146.9 0.3 maximum_convert_fusion
  147.2 2.0 %fusion.7 = bf16[256,8,512]{2,1,0:T(8,128)(2,1)} fusion(f32[258,8,512]{2,1,0:T(8,128)S(1)} %maximum_convert_fusion), kind=kLoop, calls=%fused_computation.11 | loop fusion | flops 5242880 | bytes 14680064 | tf_op jit(solution)/shard_map/convert_element_type | solution.py:80
  (18 shorter events, 0.5 us)
Async XLA Ops:
  0.0 8.8 %copy-start = (bf16[4,512,512]{2,1,0:T(8,128)(2,1)S(1)}, bf16[4,512,512]{2,1,0:T(8,128)(2,1)}, u32[]{:S(2)}) copy-start(bf16[4,512,512]{2,1,0:T(8,128)(2,1)} %param.7) | copy-start | bytes 6291460
  125.4 3.3 %copy-start.2 = (bf16[16,528,512]{2,1,0:T(8,128)(2,1)}, bf16[16,528,512]{2,1,0:T(8,128)(2,1)S(1)}, u32[]{:S(2)}) copy-start(bf16[16,528,512]{2,1,0:T(8,128)(2,1)S(1)} %all_to_all.5) | copy-start | bytes 25952260
  130.8 16.0 %collective-permute-start.1 = (bf16[1,8,512]{2,1,0:T(8,128)(2,1)S(1)}, bf16[1,8,512]{2,1,0:T(8,128)(2,1)S(1)}, u32[]{:S(2)}, u32[]{:S(2)}) collective-permute-start(bf16[1,8,512]{2,1,0:T(8,128)(2,1)S(1)} %fusion.17), channel_id=1, source_target_pairs={{16,0},{32,16},{48,32},{64,48},{80,64},{96,80},{112,96},{128,112},... | collective-permute-start | bytes 24584 | tf_op jit(solution)/shard_map/ppermute | solution.py:76
  135.2 11.7 %collective-permute-start = (bf16[1,8,512]{2,1,0:T(8,128)(2,1)S(1)}, bf16[1,8,512]{2,1,0:T(8,128)(2,1)S(1)}, u32[]{:S(2)}, u32[]{:S(2)}) collective-permute-start(bf16[1,8,512]{2,1,0:T(8,128)(2,1)S(1)} %fusion.18), channel_id=1, source_target_pairs={{0,16},{16,32},{32,48},{48,64},{64,80},{80,96},{96,112},{112,128},... | collective-permute-start | bytes 24584 | tf_op jit(solution)/shard_map/ppermute | solution.py:75
  144.5 1.6 %copy-start.1 = (bf16[256,8,512]{2,1,0:T(8,128)(2,1)S(1)}, bf16[256,8,512]{2,1,0:T(8,128)(2,1)}, u32[]{:S(2)}) copy-start(bf16[256,8,512]{2,1,0:T(8,128)(2,1)} %param.4) | copy-start | bytes 6291460
